TPU v7x, 128 devices: a whole 4x4x4 slice. The times are simulated.
128 devices in a mesh: row: 16 (over x, z_lo, core), col: 8 (over y, z_hi).
Axes of the slice: x: 4, y: 4, z: 4 (z_hi: 2, z_lo: 2; z = z_hi * 2 + z_lo), core: 2. Of those that a mesh axis runs over, the one named last changes fastest.
Arguments:
- coeffs: bfloat16 [32768, 1024], P('row', 'col'), may hold values from -6 to 6
- intersection: bfloat16 [32768, 32768], P('row', 'col'), may hold values from -0.006225586 to 0.006225586
- coeff_mask: int32 [256, 8], P('row', 'col'), may hold values 0 or 1
- intersection_mask: int32 [256, 256], P('row', 'col'), may hold values 0 or 1
Outputs:
- gradient: float32 [1024, 1024], P('row', 'col')
All inputs are finite; a program needn't handle non-finite values. No bound on the sum of `coeff_mask` or of `intersection_mask` on one device may be relied on, other than what follows from the above.
Results may differ from a plain program's by a relative error of at most 0.0029.
Values may be sent and summed in bfloat16 or wider, within the bound.
No kernel may reach another device: no remote copies, remote signals or barrier semaphores. Data moves between devices by JAX's collectives and lax.ppermute only.
A program may use at most 128 MiB of HBM per device.

v0:
```python
import jax
import jax.numpy as jnp
from jax import lax
from jax.sharding import PartitionSpec as P

BLK = 128


def mask_blocks(data, mask):
    rows, cols = data.shape
    shaped = data.reshape(rows // BLK, BLK, cols // BLK, BLK)
    return (shaped * mask.astype(data.dtype)[:, None, :, None]).reshape(rows, cols)


def local(coeffs, intersection, coeff_mask, intersection_mask):
    masked_c = mask_blocks(coeffs, coeff_mask)
    own_rows = lax.all_gather(masked_c, "col", axis=1, tiled=True)
    every_row = lax.all_gather(masked_c, "row", axis=0, tiled=True)
    far_rows = lax.all_to_all(every_row, "col", split_axis=0, concat_axis=1, tiled=True)
    masked_s = mask_blocks(intersection, intersection_mask)
    product = jnp.dot(masked_s, far_rows, preferred_element_type=jnp.float32).astype(jnp.bfloat16)
    partial_sum = lax.dot_general(
        own_rows, product, (((0,), (0,)), ((), ())), preferred_element_type=jnp.float32
    )
    halfway = lax.psum_scatter(partial_sum, "row", scatter_dimension=0, tiled=True)
    gradient = lax.psum_scatter(halfway, "col", scatter_dimension=1, tiled=True)
    return gradient


def solution(mesh):
    return jax.shard_map(
        local,
        mesh=mesh,
        in_specs=(P("row", "col"), P("row", "col"), P("row", "col"), P("row", "col")),
        out_specs=P("row", "col"),
        check_vma=False,
    )
```

profile of v0, /device:TPU:0, one launch (start us, length us, event | category | flops | bytes accessed | tf_op | source)
XLA Modules:
  0.0 396.9 jit_solution(6036179723806142665)
XLA Ops:
  7.4 0.0 all-gather.5.cloned.1.call-start
  7.4 0.7 convert_bitcast_fusion
  8.0 0.1 broadcast_bitcast_fusion
  8.1 2.2 broadcast_multiply_fusion
  10.3 0.0 all-gather.5.cloned.1.call-update
  10.3 54.7 %all-gather.5.cloned.1.call-done = bf16[32768,128]{1,0:T(8,128)(2,1)} async-done(((bf16[2048,128]{1,0:T(8,128)(2,1)}), bf16[32768,128]{1,0:T(8,128)(2,1)}) %all-gather.5.cloned.1.call-update) | async-done | bytes 8388624 | tf_op jit(solution)/shard_map/all_gather | solution.py:18
  65.1 0.0 copy-start
  65.1 6.8 %all-to-all-start = ((bf16[8,4096,128]{2,1,0:T(8,128)(2,1)}), bf16[8,4096,128]{2,1,0:T(8,128)(2,1)}, u32[]{:S(2)}, u32[]{:S(2)}) async-start(bf16[8,4096,128]{2,1,0:T(8,128)(2,1)} %bitcast.19), calls=%async_computation | async-start | bytes 16777216 | tf_op jit(solution)/shard_map/all_to_all | solution.py:19
  71.9 0.0 all-gather.3.cloned.1.call-start
  72.0 0.5 all-gather.3.cloned.1.call-update
  72.5 0.0 reduce-scatter.3.cloned.1.call-start
  72.5 0.0 copy-done
  72.6 123.9 %all-to-all-done = bf16[8,4096,128]{2,1,0:T(8,128)(2,1)} async-done(((bf16[8,4096,128]{2,1,0:T(8,128)(2,1)}), bf16[8,4096,128]{2,1,0:T(8,128)(2,1)}, u32[]{:S(2)}, u32[]{:S(2)}) %all-to-all-start) | async-done | bytes 8388640 | tf_op jit(solution)/shard_map/all_to_all | solution.py:19
  196.4 12.0 %copy.5 = bf16[4096,8,128]{0,2,1:T(8,128)(2,1)} copy(bf16[4096,8,128]{2,0,1:T(8,128)(2,1)} %bitcast.3) | data formatting | bytes 16777216 | tf_op jit(solution)/shard_map/all_to_all | solution.py:19
  208.4 3.4 all-gather.3.cloned.1.call-done
  211.8 6.2 %mul.33 = bf16[16,128,32,128]{3,2,1,0:T(8,128)(2,1)} broadcast(bf16[16,32]{1,0:T(8,128)(2,1)S(1)} %convert_element_type.10), dimensions={0,2} | broadcast | bytes 16778240 | tf_op jit(solution)/shard_map/mul | solution.py:12
  218.1 34.8 %fusion.2 = f32[1024,1024]{1,0:T(8,128)} fusion(bf16[2048,1024]{1,0:T(8,128)(2,1)} %all-gather.3.cloned.1.call-done, bf16[4096,1024]{0,1:T(8,128)(2,1)} %bitcast.20, bf16[2048,4096]{1,0:T(8,128)(2,1)} %param.5, bf16[256,8,32,128]{3,2,1,0:T(8,128)(2,1)} %bitcast.18), kind=kOutput, calls=%fused_computation.3 | convolution fusion | flops 21485322240 | bytes 50331648 | tf_op jit(solution)/shard_map/dot_general | solution.py:22
  252.9 0.0 reduce-scatter.3.cloned.1.call-update
  252.9 0.0 reduce-scatter.5.cloned.1.call-start
  253.0 66.5 %reduce-scatter.3.cloned.1.call-done = f32[64,1024]{1,0:T(8,128)} async-done(((f32[1024,1024]{1,0:T(8,128)}), f32[64,1024]{1,0:T(8,128)}) %reduce-scatter.3.cloned.1.call-update) | async-done | bytes 262160 | tf_op jit(solution)/shard_map/reduce_scatter | solution.py:25
  319.5 0.0 reduce-scatter.5.cloned.1.call-update
  319.5 70.0 %reduce-scatter.5.cloned.1.call-done = f32[64,128]{1,0:T(8,128)} async-done(((f32[64,1024]{1,0:T(8,128)}), f32[64,128]{1,0:T(8,128)}) %reduce-scatter.5.cloned.1.call-update) | async-done | bytes 32784 | tf_op jit(solution)/shard_map/reduce_scatter | solution.py:26
  (1 shorter events, 0.0 us)
Async XLA Ops:
  7.4 57.7 %all-gather.5.cloned.1.call-start = ((), (), s32[]{:S(2)}) async-start(), calls=%async_computation.4 | async-start | bytes 8912896 | tf_op jit(solution)/shard_map/all_gather | solution.py:18
  65.1 7.5 %copy-start = (s32[16,32]{1,0:T(8,128)S(1)}, s32[16,32]{1,0:T(8,128)}, u32[]{:S(2)}) copy-start(s32[16,32]{1,0:T(8,128)} %param.7) | copy-start | bytes 6148
  65.1 131.4 %all-to-all-start = ((bf16[8,4096,128]{2,1,0:T(8,128)(2,1)}), bf16[8,4096,128]{2,1,0:T(8,128)(2,1)}, u32[]{:S(2)}, u32[]{:S(2)}) async-start(bf16[8,4096,128]{2,1,0:T(8,128)(2,1)} %bitcast.19), calls=%async_computation | async-start | bytes 16777216 | tf_op jit(solution)/shard_map/all_to_all | solution.py:19
  71.9 139.9 %all-gather.3.cloned.1.call-start = ((), (), s32[]{:S(2)}) async-start(), calls=%async_computation.3 | async-start | bytes 4718592 | tf_op jit(solution)/shard_map/all_gather | solution.py:17
  72.5 247.0 %reduce-scatter.3.cloned.1.call-start = ((), (), s32[]{:S(2)}) async-start(), calls=%async_computation.5 | async-start | bytes 4456448 | tf_op jit(solution)/shard_map/reduce_scatter | solution.py:25
  252.9 136.6 %reduce-scatter.5.cloned.1.call-start = ((), (), s32[]{:S(2)}) async-start(), calls=%async_computation.6 | async-start | bytes 294912 | tf_op jit(solution)/shard_map/reduce_scatter | solution.py:26
Sparse Core Ops, SparseCore 0:
  10.4 54.5 all-gather.4
  253.0 66.4 reduce-scatter.2
Sparse Core Ops, SparseCore 1:
  74.6 137.2 all-gather.2
  319.6 69.8 reduce-scatter.4
where the time goes:
time: 397 us
  waiting for transfers between devices  319 us (80%)
  matrix products  34.8 us (9%)
  local copies, waits for them, and re-layouts  18.3 us (5%)
  between operations  14.9 us (4%)
  starting transfers between devices  6.97 us (2%)
    all_to_all x1, waiting for transfers between devices, local(): lax.all_to_all(every_row, 'col', split_axis=0, concat_axis=1, tiled=True)  124 us
    reduce_scatter x1, waiting for transfers between devices, local(): gradient = lax.psum_scatter(halfway, 'col', scatter_dimension=1, tiled=True)  70 us
    reduce_scatter x1, waiting for transfers between devices, local(): lax.psum_scatter(partial_sum, 'row', scatter_dimension=0, tiled=True)  66.5 us
    all_gather x1, waiting for transfers between devices, local(): every_row = lax.all_gather(masked_c, 'row', axis=0, tiled=True)  54.7 us
    dot_general x1, matrix products, local(): lax.dot_general(own_rows, product, (((0,), (0,)), ((), ())), preferred_el...  34.8 us
    all_to_all x1, local copies, waits for them, and re-layouts, local(): lax.all_to_all(every_row, 'col', split_axis=0, concat_axis=1, tiled=True)  12 us
  transfers between devices with their start and end apart: 5, of which 5 were waited for; matrix products, arithmetic and copies ran while one was open for 3% of the time, Pallas kernels for 0%

commit v1 on v0

v1 whole, which is shorter than its diff:
```python
import jax
import jax.numpy as jnp
from jax import lax
from jax.sharding import PartitionSpec as P

BLK = 128


def mask_blocks(data, mask):
    rows, cols = data.shape
    shaped = data.reshape(rows // BLK, BLK, cols // BLK, BLK)
    return (shaped * mask.astype(data.dtype)[:, None, :, None]).reshape(rows, cols)


def make_local(n_row, n_col):
    ratio = n_row // n_col

    perm = []
    for src_r in range(n_row):
        for o in range(n_col):
            g, h = divmod(src_r, ratio)
            dst_r = h * n_col + o
            perm.append((src_r * n_col + o, dst_r * n_col + g))

    def local(coeffs, intersection, coeff_mask, intersection_mask):
        masked_c = mask_blocks(coeffs, coeff_mask)
        rows, width = masked_c.shape
        own_rows = lax.all_gather(masked_c, "col", axis=1, tiled=True)
        moved = lax.ppermute(masked_c, ("row", "col"), perm)
        gathered = lax.all_gather(moved, "row", axis=0, tiled=False)
        group_c = (
            gathered.reshape(ratio, n_col, rows, width)
            .transpose(0, 2, 1, 3)
            .reshape(ratio * rows, n_col * width)
        )
        masked_s = mask_blocks(intersection, intersection_mask)
        product = jnp.dot(masked_s, group_c, preferred_element_type=jnp.float32).astype(jnp.bfloat16)
        pieces = product.reshape(rows, n_col, width).transpose(1, 0, 2)
        pieces = lax.all_to_all(pieces, "col", 0, 0, tiled=True)
        summed = jnp.sum(pieces.astype(jnp.float32), axis=0)
        high = summed.astype(jnp.bfloat16)
        low = (summed - high.astype(jnp.float32)).astype(jnp.bfloat16)
        both = jnp.concatenate([high, low], axis=1)
        partial = lax.dot_general(
            own_rows, both, (((0,), (0,)), ((), ())), preferred_element_type=jnp.float32
        )
        partial = partial[:, :width] + partial[:, width:]
        return lax.psum_scatter(partial, "row", scatter_dimension=0, tiled=True)

    return local


def solution(mesh):
    return jax.shard_map(
        make_local(mesh.shape["row"], mesh.shape["col"]),
        mesh=mesh,
        in_specs=(P("row", "col"), P("row", "col"), P("row", "col"), P("row", "col")),
        out_specs=P("row", "col"),
        check_vma=False,
    )
```

time: 397 us -> 283 us (0.71)
  waiting for transfers between devices: 319 us -> 151 us
  blocking collectives: 0 us -> 66.4 us
  starting transfers between devices: 6.97 us -> 0.78 us
  matrix products: 34.8 us -> 29.4 us
    all_to_all x1 -> x0, waiting for transfers between devices: 124 us -> none  [local(): lax.all_to_all(every_row, 'col', split_axis=0, concat_axis=1, tiled=True)]
    reduce_scatter x2 -> x1, waiting for transfers between devices: 137 us -> 62.2 us  [local(): return lax.psum_scatter(partial, 'row', scatter_dimension=0, tiled=True)]
    all_to_all x0 -> x1, blocking collectives: none -> 66.4 us  [local(): pieces = lax.all_to_all(pieces, 'col', 0, 0, tiled=True)]
    all_gather x1, waiting for transfers between devices: 54.7 us -> 74.4 us  [local(): gathered = lax.all_gather(moved, 'row', axis=0, tiled=False)]
    all_to_all x1 -> x0, local copies, waits for them, and re-layouts: 12 us -> none  [local(): lax.all_to_all(every_row, 'col', split_axis=0, concat_axis=1, tiled=True)]
    reshape x0 -> x1, local copies, waits for them, and re-layouts: none -> 10.4 us  [local(): gathered.reshape(ratio, n_col, rows, width).transpose(0, 2, 1, 3)]
    all_gather x1, waiting for transfers between devices: 3.41 us -> 13.5 us  [local(): own_rows = lax.all_gather(masked_c, 'col', axis=1, tiled=True)]
    all_to_all x1 -> x0, starting transfers between devices: 6.85 us -> none  [local(): lax.all_to_all(every_row, 'col', split_axis=0, concat_axis=1, tiled=True)]
  transfers between devices with their start and end apart: 5 -> 4, of which waited for: 5 -> 3; matrix products, arithmetic and copies ran while one was open for 3% -> 16% of each run, Pallas kernels for 0% -> 0%
where the time goes in v1:
time: 283 us; the launch traced here: 282 us
  waiting for transfers between devices  151 us (53%)
  blocking collectives  66.4 us (23%)
  matrix products  29.4 us (10%)
  local copies, waits for them, and re-layouts  17.5 us (6%)
  between operations  13.2 us (5%)
  other arithmetic  4.43 us (2%)
    all_gather x1, waiting for transfers between devices, local(): gathered = lax.all_gather(moved, 'row', axis=0, tiled=False)  74.4 us
    all_to_all x1, blocking collectives, local(): pieces = lax.all_to_all(pieces, 'col', 0, 0, tiled=True)  66.4 us
    reduce_scatter x1, waiting for transfers between devices, local(): return lax.psum_scatter(partial, 'row', scatter_dimension=0, tiled=True)  62.2 us
    dot_general x1, matrix products, local(): jnp.dot(masked_s, group_c, preferred_element_type=jnp.float32)  25.9 us
    all_gather x1, waiting for transfers between devices, local(): own_rows = lax.all_gather(masked_c, 'col', axis=1, tiled=True)  13.5 us
    reshape x1, local copies, waits for them, and re-layouts, local(): gathered.reshape(ratio, n_col, rows, width).transpose(0, 2, 1, 3)  10.4 us
    mul x2, local copies, waits for them, and re-layouts, mask_blocks(): shaped * mask.astype(data.dtype)[:, None, :, None]  6.3 us
  transfers between devices with their start and end apart: 4, of which 3 were waited for; matrix products, arithmetic and copies ran while one was open for 16% of the time, Pallas kernels for 0%

profile of v1, /device:TPU:0, one launch (start us, length us, event | category | flops | bytes accessed | tf_op | source)
XLA Modules:
  0.0 282.5 jit_solution(12091335025374039532)
XLA Ops:
  6.5 0.0 all-gather.6.cloned.1.call-start
  6.5 0.7 convert_bitcast_fusion
  7.2 0.1 broadcast_bitcast_fusion
  7.3 1.4 broadcast_multiply_fusion
  8.7 0.0 copy-start
  8.7 0.7 collective-permute-start
  9.4 0.0 collective-permute-done
  9.4 0.0 copy-start.1
  9.4 0.8 copy-done.1
  10.2 0.0 all-gather.6.cloned.1.call-update
  10.2 0.0 all-gather.4.cloned.1.call-start
  10.3 0.0 copy-done
  10.3 0.7 all-gather.4.cloned.1.call-update
  11.0 0.0 reduce-scatter.2.cloned.1.call-start
  11.0 0.7 convert_element_type.22
  11.7 74.4 %all-gather.6.cloned.1.call-done = bf16[32768,128]{1,0:T(8,128)(2,1)} async-done(((bf16[2048,128]{1,0:T(8,128)(2,1)}), bf16[32768,128]{1,0:T(8,128)(2,1)}) %all-gather.6.cloned.1.call-update) | async-done | bytes 8388624 | tf_op jit(solution)/shard_map/all_gather | solution.py:30
  86.1 10.4 %copy.6 = bf16[2,8,2048,128]{3,1,2,0:T(8,128)(2,1)} copy(bf16[2,8,2048,128]{3,2,1,0:T(8,128)(2,1)} %bitcast.25) | data formatting | bytes 16777216 | tf_op jit(solution)/shard_map/reshape | solution.py:32
  96.5 6.2 %mul.33 = bf16[16,128,32,128]{3,2,1,0:T(8,128)(2,1)} broadcast(bf16[16,32]{1,0:T(8,128)(2,1)S(1)} %convert_element_type.22), dimensions={0,2} | broadcast | bytes 16778240 | tf_op jit(solution)/shard_map/mul | solution.py:12
  102.7 25.9 %fusion.4 = bf16[2048,1024]{0,1:T(8,128)(2,1)} fusion(bf16[512,8,8,128]{3,2,1,0:T(8,128)(2,1)} %bitcast.26, bf16[2048,4096]{1,0:T(8,128)(2,1)} %param.5, bf16[256,8,32,128]{3,2,1,0:T(8,128)(2,1)} %bitcast.24), kind=kOutput, calls=%fused_computation.6 | convolution fusion | flops 17190354944 | bytes 46137344 | tf_op jit(solution)/shard_map/dot_general | solution.py:37
  128.6 66.4 %all_to_all.5 = bf16[8,2048,128]{1,2,0:T(8,128)(2,1)S(1)} all-to-all(bf16[8,2048,128]{1,2,0:T(8,128)(2,1)} %bitcast.27), channel_id=1, replica_groups=mesh['row'=16,'col'=8] {'col'}, dimensions={0} | all-to-all | bytes 8388608 | tf_op jit(solution)/shard_map/all_to_all | solution.py:39
  195.0 0.7 convert_reduce_fusion
  195.8 0.1 subtract_convert_fusion
  195.9 13.5 %all-gather.4.cloned.1.call-done = bf16[2048,1024]{1,0:T(8,128)(2,1)} async-done(((bf16[2048,128]{1,0:T(8,128)(2,1)}), bf16[2048,1024]{1,0:T(8,128)(2,1)}) %all-gather.4.cloned.1.call-update) | async-done | bytes 4194320 | tf_op jit(solution)/shard_map/all_gather | solution.py:28
  209.4 3.5 %fusion.7 = f32[1024,256]{1,0:T(8,128)S(1)} fusion(bf16[2048,1024]{1,0:T(8,128)(2,1)} %all-gather.4.cloned.1.call-done, bf16[2048,128]{0,1:T(8,128)(2,1)S(1)} %get-tuple-element.5, bf16[2048,128]{0,1:T(8,128)(2,1)S(1)} %get-tuple-element.6), kind=kOutput, calls=%fused_computation.7 | convolution fusion | flops 1075838976 | bytes 6291456 | tf_op jit(solution)/shard_map/dot_general | solution.py:44
  212.9 0.8 slice_add_fusion
  213.7 0.0 reduce-scatter.2.cloned.1.call-update
  213.8 62.2 %reduce-scatter.2.cloned.1.call-done = f32[64,128]{1,0:T(8,128)} async-done(((f32[1024,128]{1,0:T(8,128)}), f32[64,128]{1,0:T(8,128)}) %reduce-scatter.2.cloned.1.call-update) | async-done | bytes 32784 | tf_op jit(solution)/shard_map/reduce_scatter | solution.py:48
Async XLA Ops:
  6.5 79.6 %all-gather.6.cloned.1.call-start = ((), (), s32[]{:S(2)}) async-start(), calls=%async_computation.4 | async-start | bytes 8912896 | tf_op jit(solution)/shard_map/all_gather | solution.py:30
  8.7 1.6 copy-start
  8.7 0.7 collective-permute-start
  9.4 0.8 copy-start.1
  10.2 199.2 %all-gather.4.cloned.1.call-start = ((), (), s32[]{:S(2)}) async-start(), calls=%async_computation.2 | async-start | bytes 4718592 | tf_op jit(solution)/shard_map/all_gather | solution.py:28
  11.0 265.0 %reduce-scatter.2.cloned.1.call-start = ((), (), s32[]{:S(2)}) async-start(), calls=%async_computation.3 | async-start | bytes 557056 | tf_op jit(solution)/shard_map/reduce_scatter | solution.py:48
Sparse Core Ops, SparseCore 0:
  10.3 75.7 all-gather.5
  88.3 121.0 all-gather.3
  213.9 62.0 reduce-scatter.1

commit v2 on v1

--- a/solution.py
+++ b/solution.py
@@ -28,24 +28,24 @@
         own_rows = lax.all_gather(masked_c, "col", axis=1, tiled=True)
         moved = lax.ppermute(masked_c, ("row", "col"), perm)
         gathered = lax.all_gather(moved, "row", axis=0, tiled=False)
-        group_c = (
-            gathered.reshape(ratio, n_col, rows, width)
-            .transpose(0, 2, 1, 3)
-            .reshape(ratio * rows, n_col * width)
-        )
-        masked_s = mask_blocks(intersection, intersection_mask)
-        product = jnp.dot(masked_s, group_c, preferred_element_type=jnp.float32).astype(jnp.bfloat16)
-        pieces = product.reshape(rows, n_col, width).transpose(1, 0, 2)
+        group_c = gathered.reshape(ratio, n_col, rows, width)
+        masked_s = mask_blocks(intersection, intersection_mask).reshape(rows, ratio, rows)
+        pieces = jnp.einsum(
+            "rhk,hokn->orn", masked_s, group_c, preferred_element_type=jnp.float32
+        ).astype(jnp.bfloat16)
         pieces = lax.all_to_all(pieces, "col", 0, 0, tiled=True)
         summed = jnp.sum(pieces.astype(jnp.float32), axis=0)
-        high = summed.astype(jnp.bfloat16)
-        low = (summed - high.astype(jnp.float32)).astype(jnp.bfloat16)
+        rounded = lax.reduce_precision(summed, exponent_bits=8, mantissa_bits=7)
+        high = rounded.astype(jnp.bfloat16)
+        low = (summed - rounded).astype(jnp.bfloat16)
         both = jnp.concatenate([high, low], axis=1)
         partial = lax.dot_general(
             own_rows, both, (((0,), (0,)), ((), ())), preferred_element_type=jnp.float32
         )
         partial = partial[:, :width] + partial[:, width:]
-        return lax.psum_scatter(partial, "row", scatter_dimension=0, tiled=True)
+        spread = partial.reshape(n_row, -1, width)
+        spread = lax.all_to_all(spread, "row", 0, 0, tiled=True)
+        return jnp.sum(spread, axis=0)
 
     return local
 

time: 283 us -> 235 us (0.83)
  waiting for transfers between devices: 151 us -> 63.4 us
  local copies, waits for them, and re-layouts: 17.5 us -> 34.4 us
  blocking collectives: 66.4 us -> 80.3 us
  other arithmetic: 4.43 us -> 11.3 us
    reduce_scatter x1 -> x0, waiting for transfers between devices: 62.2 us -> none  [local(): return lax.psum_scatter(partial, 'row', scatter_dimension=0, tiled=True)]
    all_gather x1, waiting for transfers between devices: 74.4 us -> 33.9 us  [local(): gathered = lax.all_gather(moved, 'row', axis=0, tiled=False)]
    mul x2 -> x3, local copies, waits for them, and re-layouts: 6.3 us -> 30.7 us  [mask_blocks(): shaped * mask.astype(data.dtype)[:, None, :, None]]
    all_gather x1, waiting for transfers between devices: 13.5 us -> 28.8 us  [local(): own_rows = lax.all_gather(masked_c, 'col', axis=1, tiled=True)]
    all_to_all x0 -> x1, blocking collectives: none -> 14.8 us  [local(): spread = lax.all_to_all(spread, 'row', 0, 0, tiled=True)]
    reshape x1 -> x0, local copies, waits for them, and re-layouts: 10.4 us -> none  [local(): gathered.reshape(ratio, n_col, rows, width).transpose(0, 2, 1, 3)]
    mul x2 -> x3, other arithmetic: 2.03 us -> 9.03 us  [mask_blocks(): shaped * mask.astype(data.dtype)[:, None, :, None]]
    unnamed x4 -> x6, local copies, waits for them, and re-layouts: 0.82 us -> 3.73 us
  transfers between devices with their start and end apart: 4 -> 3, of which waited for: 3 -> 2; matrix products, arithmetic and copies ran while one was open for 16% -> 28% of each run, Pallas kernels for 0% -> 0%
where the time goes in v2:
time: 235 us; the launch traced here: 234 us
  blocking collectives  80.3 us (34%)
  waiting for transfers between devices  63.4 us (27%)
  local copies, waits for them, and re-layouts  34.4 us (15%)
  matrix products  29.9 us (13%)
  between operations  13.5 us (6%)
  other arithmetic  11.3 us (5%)
    all_to_all x1, blocking collectives, local(): pieces = lax.all_to_all(pieces, 'col', 0, 0, tiled=True)  65.5 us
    all_gather x1, waiting for transfers between devices, local(): gathered = lax.all_gather(moved, 'row', axis=0, tiled=False)  33.9 us
    mul x3, local copies, waits for them, and re-layouts, mask_blocks(): shaped * mask.astype(data.dtype)[:, None, :, None]  30.7 us
    all_gather x1, waiting for transfers between devices, local(): own_rows = lax.all_gather(masked_c, 'col', axis=1, tiled=True)  28.8 us
    dot_general x1, matrix products, local(): jnp.einsum('rhk,hokn->orn', masked_s, group_c, preferred_element_type=jnp...  26.4 us
    all_to_all x1, blocking collectives, local(): spread = lax.all_to_all(spread, 'row', 0, 0, tiled=True)  14.8 us
    mul x3, other arithmetic, mask_blocks(): shaped * mask.astype(data.dtype)[:, None, :, None]  9.03 us
  transfers between devices with their start and end apart: 3, of which 2 were waited for; matrix products, arithmetic and copies ran while one was open for 28% of the time, Pallas kernels for 0%

profile of v2, /device:TPU:0, one launch (start us, length us, event | category | flops | bytes accessed | tf_op | source)
XLA Modules:
  0.0 233.6 jit_solution(380507198851740262)
XLA Ops:
  6.5 0.0 all-gather.6.cloned.1.call-start
  6.5 0.7 convert_bitcast_fusion
  7.2 0.1 broadcast_bitcast_fusion
  7.3 1.4 broadcast_multiply_fusion
  8.7 0.0 copy-start.1
  8.7 0.7 collective-permute-start
  9.4 0.0 collective-permute-done
  9.4 0.0 copy-start.2
  9.4 0.8 copy-done.2
  10.2 0.0 all-gather.6.cloned.1.call-update
  10.2 0.0 all-gather.4.cloned.1.call-start
  10.2 0.0 copy-done.1
  10.3 0.7 all-gather.4.cloned.1.call-update
  10.9 0.7 convert_element_type.22
  11.7 0.0 copy-start
  11.7 2.8 %mul.36 = bf16[16,128,32,128]{3,2,1,0:T(8,128)(2,1)S(1)} broadcast(bf16[16,32]{1,0:T(8,128)(2,1)S(1)} %convert_element_type.22), dimensions={0,2} | broadcast | bytes 16778240 | tf_op jit(solution)/shard_map/mul | solution.py:12
  14.5 2.9 %copy-done = bf16[2048,4096]{1,0:T(8,128)(2,1)S(1)} copy-done((bf16[2048,4096]{1,0:T(8,128)(2,1)S(1)}, bf16[2048,4096]{1,0:T(8,128)(2,1)}, u32[]{:S(2)}) %copy-start) | copy-done | bytes 16777240
  17.4 7.0 %bitcast_multiply_fusion = bf16[2048,4096]{1,0:T(8,128)(2,1)} fusion(bf16[2048,4096]{1,0:T(8,128)(2,1)S(1)} %copy-done, bf16[256,8,32,128]{3,2,1,0:T(8,128)(2,1)S(1)} %bitcast.19), kind=kLoop, calls=%fused_computation | loop fusion | flops 8388608 | bytes 50331648 | tf_op jit(solution)/shard_map/mul | solution.py:12
  24.4 27.8 %mul.39 = bf16[2048,2,2048]{2,1,0:T(2,128)(2,1)} reshape(bf16[2048,4096]{1,0:T(8,128)(2,1)} %bitcast_multiply_fusion) | data formatting | bytes 33554432 | tf_op jit(solution)/shard_map/mul | solution.py:12
  52.2 33.9 %all-gather.6.cloned.1.call-done = bf16[32768,128]{1,0:T(8,128)(2,1)} async-done(((bf16[2048,128]{1,0:T(8,128)(2,1)}), bf16[32768,128]{1,0:T(8,128)(2,1)}) %all-gather.6.cloned.1.call-update) | async-done | bytes 8388624 | tf_op jit(solution)/shard_map/all_gather | solution.py:30
  86.1 26.4 %fusion.4 = bf16[8,2048,128]{1,2,0:T(8,128)(2,1)S(1)} fusion(bf16[2,8,2048,128]{3,2,1,0:T(8,128)(2,1)} %bitcast.22, bf16[2048,2,2048,1]{2,1,0,3:T(2,128)(2,1)} %bitcast.20), kind=kOutput, calls=%fused_computation.5 | convolution fusion | flops 17181966336 | bytes 29360128 | tf_op jit(solution)/shard_map/rhk,hokn->orn/dot_general | solution.py:33
  112.6 65.5 %all_to_all.10 = bf16[8,2048,128]{1,2,0:T(8,128)(2,1)S(1)} all-to-all(bf16[8,2048,128]{1,2,0:T(8,128)(2,1)S(1)} %fusion.4), channel_id=1, replica_groups=mesh['row'=16,'col'=8] {'col'}, dimensions={0} | all-to-all | bytes 8388608 | tf_op jit(solution)/shard_map/all_to_all | solution.py:36
  178.0 0.7 convert_reduce_fusion
  178.8 0.2 reduce-precision_convert_fusion
  178.9 28.8 %all-gather.4.cloned.1.call-done = bf16[2048,1024]{1,0:T(8,128)(2,1)} async-done(((bf16[2048,128]{1,0:T(8,128)(2,1)}), bf16[2048,1024]{1,0:T(8,128)(2,1)}) %all-gather.4.cloned.1.call-update) | async-done | bytes 4194320 | tf_op jit(solution)/shard_map/all_gather | solution.py:28
  207.8 3.5 %fusion.8 = f32[1024,256]{1,0:T(8,128)S(1)} fusion(bf16[2048,1024]{1,0:T(8,128)(2,1)} %all-gather.4.cloned.1.call-done, bf16[2048,128]{0,1:T(8,128)(2,1)S(1)} %get-tuple-element.6, bf16[2048,128]{0,1:T(8,128)(2,1)S(1)} %get-tuple-element.5), kind=kOutput, calls=%fused_computation.9 | convolution fusion | flops 1075838976 | bytes 6291456 | tf_op jit(solution)/shard_map/dot_general | solution.py:42
  211.3 0.1 slice_add_fusion
  211.3 14.8 %all_to_all.11 = f32[16,64,128]{2,1,0:T(8,128)S(1)} all-to-all(f32[16,64,128]{2,1,0:T(8,128)S(1)} %bitcast.21), channel_id=1, replica_groups=mesh['row'=16,'col'=8] {'row'}, dimensions={0} | all-to-all | bytes 1048576 | tf_op jit(solution)/shard_map/all_to_all | solution.py:47
  226.1 0.6 reduce_sum.19
Async XLA Ops:
  6.5 79.6 %all-gather.6.cloned.1.call-start = ((), (), s32[]{:S(2)}) async-start(), calls=%async_computation.3 | async-start | bytes 8912896 | tf_op jit(solution)/shard_map/all_gather | solution.py:30
  8.7 1.6 copy-start.1
  8.7 0.7 collective-permute-start
  9.4 0.8 copy-start.2
  10.2 197.6 %all-gather.4.cloned.1.call-start = ((), (), s32[]{:S(2)}) async-start(), calls=%async_computation.2 | async-start | bytes 4718592 | tf_op jit(solution)/shard_map/all_gather | solution.py:28
  11.7 5.8 %copy-start = (bf16[2048,4096]{1,0:T(8,128)(2,1)S(1)}, bf16[2048,4096]{1,0:T(8,128)(2,1)}, u32[]{:S(2)}) copy-start(bf16[2048,4096]{1,0:T(8,128)(2,1)} %param.5) | copy-start | bytes 50331652
Sparse Core Ops, SparseCore 0:
  10.3 75.7 all-gather.5
  88.3 119.4 all-gather.3

commit v3 on v2

v3 whole, which is shorter than its diff:
```python
import jax
import jax.numpy as jnp
from jax import lax
from jax.sharding import Mesh
from jax.sharding import PartitionSpec as P

BLK = 128
ROW = ("rx", "rz", "rc")
COL = ("cy", "cz")
CHIPS = ("rx", "rz")


def mask_blocks(data, mask):
    rows, cols = data.shape
    shaped = data.reshape(rows // BLK, BLK, cols // BLK, BLK)
    return (shaped * mask.astype(data.dtype)[:, None, :, None]).reshape(rows, cols)


def make_local(n_row, n_col, n_core):
    ratio = n_row // n_col
    assert ratio == n_core

    perm = []
    for src_r in range(n_row):
        for o in range(n_col):
            g, h = divmod(src_r, ratio)
            dst_r = o * ratio + h
            perm.append((src_r * n_col + o, dst_r * n_col + g))

    def local(coeffs, intersection, coeff_mask, intersection_mask):
        masked_c = mask_blocks(coeffs, coeff_mask)
        rows, width = masked_c.shape
        core = lax.axis_index("rc")
        own_rows = lax.all_gather(masked_c, COL, axis=1, tiled=True)
        moved = lax.ppermute(masked_c, ROW + COL, perm)
        mine = lax.all_gather(moved, CHIPS, axis=0, tiled=False)
        other = lax.ppermute(mine, "rc", [(0, 1), (1, 0)])
        masked_s = mask_blocks(intersection, intersection_mask)
        s_mine = lax.dynamic_slice_in_dim(masked_s, core * rows, rows, axis=1)
        s_other = lax.dynamic_slice_in_dim(masked_s, (1 - core) * rows, rows, axis=1)
        pieces = jnp.einsum("rk,okn->orn", s_mine, mine, preferred_element_type=jnp.float32)
        pieces = pieces + jnp.einsum(
            "rk,okn->orn", s_other, other, preferred_element_type=jnp.float32
        )
        pieces = lax.all_to_all(pieces.astype(jnp.bfloat16), COL, 0, 0, tiled=True)
        summed = jnp.sum(pieces.astype(jnp.float32), axis=0)
        rounded = lax.reduce_precision(summed, exponent_bits=8, mantissa_bits=7)
        high = rounded.astype(jnp.bfloat16)
        low = (summed - rounded).astype(jnp.bfloat16)
        both = jnp.concatenate([high, low], axis=1)
        partial = lax.dot_general(
            own_rows, both, (((0,), (0,)), ((), ())), preferred_element_type=jnp.float32
        )
        partial = partial[:, :width] + partial[:, width:]
        spread = partial.reshape(n_row, -1, width)
        spread = lax.all_to_all(spread, ROW, 0, 0, tiled=True)
        return jnp.sum(spread, axis=0)

    return local


def solution(mesh):
    n_row, n_col = mesh.shape["row"], mesh.shape["col"]
    n_core = 2
    n_y = 4
    fine = Mesh(
        mesh.devices.reshape(n_row // (2 * n_core), 2, n_core, n_y, n_col // n_y),
        ROW + COL,
    )
    return jax.shard_map(
        make_local(n_row, n_col, n_core),
        mesh=fine,
        in_specs=(P(ROW, COL), P(ROW, COL), P(ROW, COL), P(ROW, COL)),
        out_specs=P(ROW, COL),
        check_vma=False,
    )
```

time: 235 us -> 286 us (1.22)
  waiting for transfers between devices: 63.4 us -> 132 us
  local copies, waits for them, and re-layouts: 34.4 us -> 13.2 us
    all_gather x2, waiting for transfers between devices: 62.7 us -> 132 us  [the longest x1 120 us: local(): mine = lax.all_gather(moved, CHIPS, axis=0, tiled=False)]
    mul x3 -> x2, local copies, waits for them, and re-layouts: 30.7 us -> 2.93 us  [mask_blocks(): shaped * mask.astype(data.dtype)[:, None, :, None]]
    all_gather x0 -> x1, local copies, waits for them, and re-layouts: none -> 6.54 us  [local(): mine = lax.all_gather(moved, CHIPS, axis=0, tiled=False)]
    dot_general x1 -> x2, matrix products: 26.4 us -> 28.3 us  [the longest x1 14.7 us: local(): jnp.einsum('rk,okn->orn', s_other, other, preferred_element_type=jnp.floa...]
  transfers between devices with their start and end apart: 3 -> 4, of which waited for: 2 -> 2; matrix products, arithmetic and copies ran while one was open for 28% -> 14% of each run, Pallas kernels for 0% -> 0%
where the time goes in v3:
time: 286 us; the launch traced here: 285 us
  waiting for transfers between devices  132 us (46%)
  blocking collectives  81.4 us (28%)
  matrix products  31.8 us (11%)
  between operations  15 us (5%)
  local copies, waits for them, and re-layouts  13.2 us (5%)
  other arithmetic  10.6 us (4%)
    all_gather x1, waiting for transfers between devices, local(): mine = lax.all_gather(moved, CHIPS, axis=0, tiled=False)  120 us
    all_to_all x1, blocking collectives, local(): pieces = lax.all_to_all(pieces.astype(jnp.bfloat16), COL, 0, 0, tiled=True)  65.8 us
    all_to_all x1, blocking collectives, local(): spread = lax.all_to_all(spread, ROW, 0, 0, tiled=True)  15.6 us
    dot_general x1, matrix products, local(): jnp.einsum('rk,okn->orn', s_other, other, preferred_element_type=jnp.floa...  14.7 us
    dot_general x1, matrix products, local(): jnp.einsum('rk,okn->orn', s_mine, mine, preferred_element_type=jnp.float32)  13.5 us
    all_gather x1, waiting for transfers between devices, local(): own_rows = lax.all_gather(masked_c, COL, axis=1, tiled=True)  12.4 us
    mul x3, other arithmetic, mask_blocks(): shaped * mask.astype(data.dtype)[:, None, :, None]  9.04 us
    all_gather x1, local copies, waits for them, and re-layouts, local(): mine = lax.all_gather(moved, CHIPS, axis=0, tiled=False)  6.54 us
  transfers between devices with their start and end apart: 4, of which 2 were waited for; matrix products, arithmetic and copies ran while one was open for 14% of the time, Pallas kernels for 0%

profile of v3, /device:TPU:0, one launch (start us, length us, event | category | flops | bytes accessed | tf_op | source)
XLA Modules:
  0.0 284.9 jit_solution(2587137730879399284)
XLA Ops:
  7.4 0.0 copy-start.4
  7.4 0.0 all-gather.6.cloned.1.call-start
  7.4 0.7 convert_bitcast_fusion
  8.0 0.1 broadcast_bitcast_fusion
  8.1 1.4 broadcast_multiply_fusion
  9.5 0.0 copy-start.2
  9.5 0.7 collective-permute-start
  10.2 0.0 collective-permute-done
  10.2 0.0 copy-start.3
  10.2 0.8 copy-done.3
  11.0 0.0 all-gather.6.cloned.1.call-update
  11.1 0.0 all-gather.4.cloned.1.call-start
  11.1 119.9 %all-gather.6.cloned.1.call-done = bf16[16384,128]{1,0:T(8,128)(2,1)} async-done(((bf16[2048,128]{1,0:T(8,128)(2,1)}), bf16[16384,128]{1,0:T(8,128)(2,1)}) %all-gather.6.cloned.1.call-update) | async-done | bytes 4194320 | tf_op jit(solution)/shard_map/all_gather | solution.py:36
  131.0 6.5 %copy.8 = bf16[8,2048,128]{1,2,0:T(8,128)(2,1)} copy(bf16[8,2048,128]{2,1,0:T(8,128)(2,1)} %bitcast.24) | data formatting | bytes 8388608 | tf_op jit(solution)/shard_map/all_gather | solution.py:36
  137.5 0.0 collective-permute-start.1
  137.5 0.0 copy-done.2
  137.5 0.0 all-gather.4.cloned.1.call-update
  137.5 0.0 copy-done.4
  137.6 0.0 copy-start
  137.6 2.9 %mul.39 = bf16[16,128,32,128]{3,2,1,0:T(8,128)(2,1)S(1)} broadcast(bf16[16,32]{1,0:T(8,128)(2,1)S(1)} %convert_element_type.22), dimensions={0,2} | broadcast | bytes 16778240 | tf_op jit(solution)/shard_map/mul | solution.py:16
  140.4 2.9 %copy-done = bf16[2048,4096]{1,0:T(8,128)(2,1)S(1)} copy-done((bf16[2048,4096]{1,0:T(8,128)(2,1)S(1)}, bf16[2048,4096]{1,0:T(8,128)(2,1)}, u32[]{:S(2)}) %copy-start) | copy-done | bytes 16777240
  143.3 7.0 %bitcast_multiply_fusion = bf16[2048,4096]{1,0:T(8,128)(2,1)} fusion(bf16[2048,4096]{1,0:T(8,128)(2,1)S(1)} %copy-done, bf16[256,8,32,128]{3,2,1,0:T(8,128)(2,1)S(1)} %bitcast.23), kind=kLoop, calls=%fused_computation | loop fusion | flops 8388608 | bytes 50331648 | tf_op jit(solution)/shard_map/mul | solution.py:16
  150.3 0.0 copy-start.1
  150.3 0.0 collective-permute-done.1
  150.3 14.7 %fusion = f32[8,128,2048]{2,1,0:T(8,128)} fusion(bf16[8,2048,128]{1,2,0:T(8,128)(2,1)} %collective-permute-done.1, bf16[2048,4096]{1,0:T(8,128)(2,1)} %bitcast_multiply_fusion, s32[]{:T(128)S(6)} %select_n.7), kind=kOutput, calls=%fused_computation.1 | convolution fusion | flops 8589934592 | bytes 20971524 | tf_op jit(solution)/shard_map/rk,okn->orn/dot_general | solution.py:42
  165.1 0.0 copy-done.1
  165.1 13.5 %fusion.6 = bf16[8,2048,128]{1,2,0:T(8,128)(2,1)} fusion(f32[8,128,2048]{2,1,0:T(8,128)} %fusion, bf16[8,2048,128]{2,1,0:T(8,128)(2,1)} %bitcast.25, bf16[2048,4096]{1,0:T(8,128)(2,1)S(1)} %copy-done.1, s32[]{:T(128)S(6)} %select_n.6), kind=kOutput, calls=%fused_computation.9 | convolution fusion | flops 8594128896 | bytes 25165828 | tf_op jit(solution)/shard_map/rk,okn->orn/dot_general | solution.py:41
  178.6 65.8 %all_to_all.10 = bf16[8,2048,128]{1,2,0:T(8,128)(2,1)S(1)} all-to-all(bf16[8,2048,128]{1,2,0:T(8,128)(2,1)} %fusion.6), channel_id=1, replica_groups=mesh['rx'=4,'rz'=2,'rc'=2,'cy'=4,'cz'=2] {'cy','cz'}, dimensions={0} | all-to-all | bytes 8388608 | tf_op jit(solution)/shard_map/all_to_all | solution.py:45
  244.4 0.7 convert_reduce_fusion
  245.1 0.2 reduce-precision_convert_fusion
  245.3 12.4 %all-gather.4.cloned.1.call-done = bf16[2048,1024]{1,0:T(8,128)(2,1)} async-done(((bf16[2048,128]{1,0:T(8,128)(2,1)}), bf16[2048,1024]{1,0:T(8,128)(2,1)}) %all-gather.4.cloned.1.call-update) | async-done | bytes 4194320 | tf_op jit(solution)/shard_map/all_gather | solution.py:34
  257.7 3.5 %fusion.10 = f32[1024,256]{1,0:T(8,128)S(1)} fusion(bf16[2048,1024]{1,0:T(8,128)(2,1)} %all-gather.4.cloned.1.call-done, bf16[2048,128]{0,1:T(8,128)(2,1)S(1)} %get-tuple-element.6, bf16[2048,128]{0,1:T(8,128)(2,1)S(1)} %get-tuple-element.5), kind=kOutput, calls=%fused_computation.13 | convolution fusion | flops 1075838976 | bytes 6291456 | tf_op jit(solution)/shard_map/dot_general | solution.py:51
  261.2 0.1 slice_add_fusion
  261.2 15.6 %all_to_all.11 = f32[16,64,128]{2,1,0:T(8,128)S(1)} all-to-all(f32[16,64,128]{2,1,0:T(8,128)S(1)} %bitcast.26), channel_id=1, replica_groups=mesh['rx'=4,'rz'=2,'rc'=2,'cy'=4,'cz'=2] {'rx','rz','rc'}, dimensions={0} | all-to-all | bytes 1048576 | tf_op jit(solution)/shard_map/all_to_all | solution.py:56
  276.8 0.6 reduce_sum.19
  (1 shorter events, 0.0 us)
Async XLA Ops:
  7.4 130.2 %copy-start.4 = (s32[16,32]{1,0:T(8,128)S(1)}, s32[16,32]{1,0:T(8,128)}, u32[]{:S(2)}) copy-start(s32[16,32]{1,0:T(8,128)} %param.7) | copy-start | bytes 6148
  7.4 123.6 %all-gather.6.cloned.1.call-start = ((), (), s32[]{:S(2)}) async-start(), calls=%async_computation.3 | async-start | bytes 4718592 | tf_op jit(solution)/shard_map/all_gather | solution.py:36
  9.5 128.0 %copy-start.2 = (bf16[2048,128]{1,0:T(8,128)(2,1)}, bf16[2048,128]{1,0:T(8,128)(2,1)S(1)}, u32[]{:S(2)}) copy-start(bf16[2048,128]{1,0:T(8,128)(2,1)S(1)} %broadcast_multiply_fusion) | copy-start | bytes 1572868
  9.5 0.7 collective-permute-start
  10.2 0.8 copy-start.3
  11.1 246.6 %all-gather.4.cloned.1.call-start = ((), (), s32[]{:S(2)}) async-start(), calls=%async_computation.2 | async-start | bytes 4718592 | tf_op jit(solution)/shard_map/all_gather | solution.py:34
  137.5 12.8 %collective-permute-start.1 = (bf16[8,2048,128]{1,2,0:T(8,128)(2,1)}, bf16[8,2048,128]{1,2,0:T(8,128)(2,1)}, u32[]{:S(2)}, u32[]{:S(2)}) collective-permute-start(bf16[8,2048,128]{1,2,0:T(8,128)(2,1)} %copy.8), channel_id=1, source_target_pairs={{0,8},{8,0},{1,9},{9,1},{2,10},{10,2},{3,11},{11,3},{4,12},{12,4},... | collective-permute-start | bytes 12582920 | tf_op jit(solution)/shard_map/ppermute | solution.py:37
  137.6 5.8 %copy-start = (bf16[2048,4096]{1,0:T(8,128)(2,1)S(1)}, bf16[2048,4096]{1,0:T(8,128)(2,1)}, u32[]{:S(2)}) copy-start(bf16[2048,4096]{1,0:T(8,128)(2,1)} %param.5) | copy-start | bytes 50331652
  150.3 14.8 %copy-start.1 = (bf16[2048,4096]{1,0:T(8,128)(2,1)S(1)}, bf16[2048,4096]{1,0:T(8,128)(2,1)}, u32[]{:S(2)}) copy-start(bf16[2048,4096]{1,0:T(8,128)(2,1)} %bitcast_multiply_fusion) | copy-start | bytes 50331652
Sparse Core Ops, SparseCore 0:
  11.2 119.7 all-gather.5
Sparse Core Ops, SparseCore 1:
  137.6 120.0 all-gather.3

commit v4 on v2

--- a/solution.py
+++ b/solution.py
@@ -33,8 +33,12 @@
         pieces = jnp.einsum(
             "rhk,hokn->orn", masked_s, group_c, preferred_element_type=jnp.float32
         ).astype(jnp.bfloat16)
-        pieces = lax.all_to_all(pieces, "col", 0, 0, tiled=True)
-        summed = jnp.sum(pieces.astype(jnp.float32), axis=0)
+        me = lax.axis_index("col")
+        summed = lax.dynamic_index_in_dim(pieces, me, 0, keepdims=False).astype(jnp.float32)
+        for k in range(1, n_col):
+            out = lax.dynamic_index_in_dim(pieces, (me + k) % n_col, 0, keepdims=False)
+            got = lax.ppermute(out, "col", [(c, (c + k) % n_col) for c in range(n_col)])
+            summed = summed + got.astype(jnp.float32)
         rounded = lax.reduce_precision(summed, exponent_bits=8, mantissa_bits=7)
         high = rounded.astype(jnp.bfloat16)
         low = (summed - rounded).astype(jnp.bfloat16)

time: 235 us -> 233 us (level)
  blocking collectives: 80.3 us -> 16.6 us
  starting transfers between devices: 0.74 us -> 41.3 us
  waiting for transfers between devices: 63.4 us -> 78.7 us
  local copies, waits for them, and re-layouts: 34.4 us -> 37.6 us
    all_to_all x1 -> x0, blocking collectives: 65.5 us -> none  [local(): pieces = lax.all_to_all(pieces, 'col', 0, 0, tiled=True)]
    ppermute x0 -> x7, starting transfers between devices: none -> 40.6 us  [local(): got = lax.ppermute(out, 'col', [(c, (c + k) % n_col) for c in range(n_col)])]
    ppermute x0 -> x7, waiting for transfers between devices: none -> 33.4 us  [local(): got = lax.ppermute(out, 'col', [(c, (c + k) % n_col) for c in range(n_col)])]
    all_gather x1, waiting for transfers between devices: 28.8 us -> 10.7 us  [local(): own_rows = lax.all_gather(masked_c, 'col', axis=1, tiled=True)]
    unnamed x6 -> x8, local copies, waits for them, and re-layouts: 3.73 us -> 5.69 us
  transfers between devices with their start and end apart: 3 -> 10, of which waited for: 2 -> 7; matrix products, arithmetic and copies ran while one was open for 28% -> 30% of each run, Pallas kernels for 0% -> 0%
where the time goes in v4:
time: 233 us; the launch traced here: 231 us
  waiting for transfers between devices  78.7 us (34%)
  starting transfers between devices  41.3 us (18%)
  local copies, waits for them, and re-layouts  37.6 us (16%)
  matrix products  29.9 us (13%)
  blocking collectives  16.6 us (7%)
  between operations  13.5 us (6%)
  other arithmetic  13 us (6%)
    ppermute x7, starting transfers between devices, local(): got = lax.ppermute(out, 'col', [(c, (c + k) % n_col) for c in range(n_col)])  40.6 us
    all_gather x1, waiting for transfers between devices, local(): gathered = lax.all_gather(moved, 'row', axis=0, tiled=False)  33.9 us
    ppermute x7, waiting for transfers between devices, local(): got = lax.ppermute(out, 'col', [(c, (c + k) % n_col) for c in range(n_col)])  33.4 us
    mul x3, local copies, waits for them, and re-layouts, mask_blocks(): shaped * mask.astype(data.dtype)[:, None, :, None]  30.7 us
    dot_general x1, matrix products, local(): jnp.einsum('rhk,hokn->orn', masked_s, group_c, preferred_element_type=jnp...  26.4 us
    all_to_all x1, blocking collectives, local(): spread = lax.all_to_all(spread, 'row', 0, 0, tiled=True)  16.6 us
    all_gather x1, waiting for transfers between devices, local(): own_rows = lax.all_gather(masked_c, 'col', axis=1, tiled=True)  10.7 us
    mul x3, other arithmetic, mask_blocks(): shaped * mask.astype(data.dtype)[:, None, :, None]  9.03 us
  transfers between devices with their start and end apart: 10, of which 7 were waited for; matrix products, arithmetic and copies ran while one was open for 30% of the time, Pallas kernels for 0%

profile of v4, /device:TPU:0, one launch (start us, length us, event | category | flops | bytes accessed | tf_op | source)
XLA Modules:
  0.0 230.6 jit_solution(10105798032769823468)
XLA Ops:
  6.5 0.0 all-gather.6.cloned.1.call-start
  6.5 0.7 convert_bitcast_fusion
  7.2 0.1 broadcast_bitcast_fusion
  7.3 1.4 broadcast_multiply_fusion
  8.7 0.0 copy-start.2
  8.7 0.7 collective-permute-start
  9.4 0.0 collective-permute-done
  9.4 0.0 copy-start.3
  9.4 0.8 copy-done.3
  10.2 0.0 all-gather.6.cloned.1.call-update
  10.2 0.0 all-gather.4.cloned.1.call-start
  10.2 0.0 copy-done.2
  10.3 0.7 all-gather.4.cloned.1.call-update
  10.9 0.7 convert_element_type.47
  11.6 0.0 copy-start
  11.7 2.8 %mul.36 = bf16[16,128,32,128]{3,2,1,0:T(8,128)(2,1)S(1)} broadcast(bf16[16,32]{1,0:T(8,128)(2,1)S(1)} %convert_element_type.47), dimensions={0,2} | broadcast | bytes 16778240 | tf_op jit(solution)/shard_map/mul | solution.py:12
  14.5 2.9 %copy-done = bf16[2048,4096]{1,0:T(8,128)(2,1)S(1)} copy-done((bf16[2048,4096]{1,0:T(8,128)(2,1)S(1)}, bf16[2048,4096]{1,0:T(8,128)(2,1)}, u32[]{:S(2)}) %copy-start) | copy-done | bytes 16777240
  17.4 7.0 %bitcast_multiply_fusion = bf16[2048,4096]{1,0:T(8,128)(2,1)} fusion(bf16[2048,4096]{1,0:T(8,128)(2,1)S(1)} %copy-done, bf16[256,8,32,128]{3,2,1,0:T(8,128)(2,1)S(1)} %bitcast.60), kind=kLoop, calls=%fused_computation | loop fusion | flops 8388608 | bytes 50331648 | tf_op jit(solution)/shard_map/mul | solution.py:12
  24.4 27.8 %mul.39 = bf16[2048,2,2048]{2,1,0:T(2,128)(2,1)} reshape(bf16[2048,4096]{1,0:T(8,128)(2,1)} %bitcast_multiply_fusion) | data formatting | bytes 33554432 | tf_op jit(solution)/shard_map/mul | solution.py:12
  52.2 33.9 %all-gather.6.cloned.1.call-done = bf16[32768,128]{1,0:T(8,128)(2,1)} async-done(((bf16[2048,128]{1,0:T(8,128)(2,1)}), bf16[32768,128]{1,0:T(8,128)(2,1)}) %all-gather.6.cloned.1.call-update) | async-done | bytes 8388624 | tf_op jit(solution)/shard_map/all_gather | solution.py:30
  86.1 26.4 %bitcast_convert_fusion = bf16[8,128,2048]{2,1,0:T(8,128)(2,1)S(1)} fusion(bf16[2,8,2048,128]{3,2,1,0:T(8,128)(2,1)} %bitcast.63, bf16[2048,2,2048,1]{2,1,0,3:T(2,128)(2,1)} %bitcast.61), kind=kOutput, calls=%fused_computation.3 | convolution fusion | flops 17181966336 | bytes 29360128 | tf_op jit(solution)/shard_map/rhk,hokn->orn/dot_general | solution.py:33
  112.5 0.0 copy-start.1
  112.6 2.0 copy-done.1
  114.5 1.2 dynamic-slice_bitcast_fusion.6
  115.7 3.0 %collective-permute-start.1 = (bf16[2048,128]{0,1:T(8,128)(2,1)S(1)}, bf16[2048,128]{0,1:T(8,128)(2,1)S(1)}, u32[]{:S(2)}, u32[]{:S(2)}) collective-permute-start(bf16[2048,128]{0,1:T(8,128)(2,1)S(1)} %get-tuple-element.7), channel_id=1, source_target_pairs={{0,1},{1,2},{2,3},{3,4},{4,5},{5,6},{6,7},{7,0},{8,9},{9,10},{10,1... | collective-permute-start | bytes 1572872 | tf_op jit(solution)/shard_map/ppermute | solution.py:40
  118.7 1.5 collective-permute-start.2
  120.2 2.1 collective-permute-start.3
  122.2 2.1 collective-permute-start.4
  124.3 4.5 %collective-permute-start.5 = (bf16[2048,128]{0,1:T(8,128)(2,1)S(1)}, bf16[2048,128]{0,1:T(8,128)(2,1)}, u32[]{:S(2)}, u32[]{:S(2)}) collective-permute-start(bf16[2048,128]{0,1:T(8,128)(2,1)S(1)} %get-tuple-element.10), channel_id=1, source_target_pairs={{0,5},{1,6},{2,7},{3,0},{4,1},{5,2},{6,3},{7,4},{8,13},{9,14},{10,... | collective-permute-start | bytes 1572872 | tf_op jit(solution)/shard_map/ppermute | solution.py:40
  128.8 9.6 %collective-permute-done.1 = bf16[2048,128]{0,1:T(8,128)(2,1)S(1)} collective-permute-done((bf16[2048,128]{0,1:T(8,128)(2,1)S(1)}, bf16[2048,128]{0,1:T(8,128)(2,1)S(1)}, u32[]{:S(2)}, u32[]{:S(2)}) %collective-permute-start.1) | collective-permute-done | bytes 524320 | tf_op jit(solution)/shard_map/ppermute | solution.py:40
  138.4 7.3 %collective-permute-start.6 = (bf16[2048,128]{0,1:T(8,128)(2,1)S(1)}, bf16[2048,128]{0,1:T(8,128)(2,1)}, u32[]{:S(2)}, u32[]{:S(2)}) collective-permute-start(bf16[2048,128]{0,1:T(8,128)(2,1)S(1)} %get-tuple-element.9), channel_id=1, source_target_pairs={{0,6},{1,7},{2,0},{3,1},{4,2},{5,3},{6,4},{7,5},{8,14},{9,15},{10,... | collective-permute-start | bytes 1572872 | tf_op jit(solution)/shard_map/ppermute | solution.py:40
  145.6 0.0 collective-permute-done.2
  145.7 20.2 %collective-permute-start.7 = (bf16[2048,128]{0,1:T(8,128)(2,1)S(1)}, bf16[2048,128]{0,1:T(8,128)(2,1)}, u32[]{:S(2)}, u32[]{:S(2)}) collective-permute-start(bf16[2048,128]{0,1:T(8,128)(2,1)S(1)} %get-tuple-element.8), channel_id=1, source_target_pairs={{0,7},{1,0},{2,1},{3,2},{4,3},{5,4},{6,5},{7,6},{8,15},{9,8},{10,9... | collective-permute-start | bytes 1572872 | tf_op jit(solution)/shard_map/ppermute | solution.py:40
  165.8 6.5 %collective-permute-done.3 = bf16[2048,128]{0,1:T(8,128)(2,1)} collective-permute-done((bf16[2048,128]{0,1:T(8,128)(2,1)}, bf16[2048,128]{0,1:T(8,128)(2,1)}, u32[]{:S(2)}, u32[]{:S(2)}) %collective-permute-start.3) | collective-permute-done | bytes 524320 | tf_op jit(solution)/shard_map/ppermute | solution.py:40
  172.4 1.3 collective-permute-done.4
  173.7 13.1 %collective-permute-done.5 = bf16[2048,128]{0,1:T(8,128)(2,1)} collective-permute-done((bf16[2048,128]{0,1:T(8,128)(2,1)S(1)}, bf16[2048,128]{0,1:T(8,128)(2,1)}, u32[]{:S(2)}, u32[]{:S(2)}) %collective-permute-start.5) | collective-permute-done | bytes 524320 | tf_op jit(solution)/shard_map/ppermute | solution.py:40
  186.7 0.0 collective-permute-done.6
  186.7 3.0 %collective-permute-done.7 = bf16[2048,128]{0,1:T(8,128)(2,1)} collective-permute-done((bf16[2048,128]{0,1:T(8,128)(2,1)S(1)}, bf16[2048,128]{0,1:T(8,128)(2,1)}, u32[]{:S(2)}, u32[]{:S(2)}) %collective-permute-start.7) | collective-permute-done | bytes 524320 | tf_op jit(solution)/shard_map/ppermute | solution.py:40
  189.7 2.5 %reduce-precision_convert_fusion = (bf16[2048,128]{0,1:T(8,128)(2,1)S(1)}, f32[2048,128]{0,1:T(8,128)S(1)}) fusion(bf16[2048,128]{0,1:T(8,128)(2,1)} %collective-permute-done.7, bf16[2048,128]{0,1:T(8,128)(2,1)} %collective-permute-done.6, bf16[2048,128]{0,1:T(8,128)(2,1)} %collective-permute-done.5, bf16[2048,128]{0,1:T(8,128)(2,1)} %collective-permute-done.4, ...), kind=kLoop, calls=%fused_computation.5 | loop fusion | flops 4456448 | bytes 5767172 | tf_op jit(solution)/shard_map/convert_element_type | solution.py:43
  192.2 0.1 fusion.4
  192.3 10.7 %all-gather.4.cloned.1.call-done = bf16[2048,1024]{1,0:T(8,128)(2,1)} async-done(((bf16[2048,128]{1,0:T(8,128)(2,1)}), bf16[2048,1024]{1,0:T(8,128)(2,1)}) %all-gather.4.cloned.1.call-update) | async-done | bytes 4194320 | tf_op jit(solution)/shard_map/all_gather | solution.py:28
  203.0 3.5 %fusion.5 = f32[1024,256]{1,0:T(8,128)S(1)} fusion(bf16[2048,1024]{1,0:T(8,128)(2,1)} %all-gather.4.cloned.1.call-done, bf16[2048,128]{0,1:T(8,128)(2,1)S(1)} %fusion.4, bf16[2048,128]{0,1:T(8,128)(2,1)S(1)} %get-tuple-element.5), kind=kOutput, calls=%fused_computation.7 | convolution fusion | flops 1075838976 | bytes 6291456 | tf_op jit(solution)/shard_map/dot_general | solution.py:46
  206.5 0.1 slice_add_fusion
  206.6 16.6 %all_to_all.5 = f32[16,64,128]{2,1,0:T(8,128)S(1)} all-to-all(f32[16,64,128]{2,1,0:T(8,128)S(1)} %bitcast.62), channel_id=1, replica_groups=mesh['row'=16,'col'=8] {'row'}, dimensions={0} | all-to-all | bytes 1048576 | tf_op jit(solution)/shard_map/all_to_all | solution.py:51
  223.1 0.6 reduce_sum.9
Async XLA Ops:
  6.5 79.6 %all-gather.6.cloned.1.call-start = ((), (), s32[]{:S(2)}) async-start(), calls=%async_computation.2 | async-start | bytes 8912896 | tf_op jit(solution)/shard_map/all_gather | solution.py:30
  8.7 1.6 copy-start.2
  8.7 0.7 collective-permute-start
  9.4 0.8 copy-start.3
  10.2 192.8 %all-gather.4.cloned.1.call-start = ((), (), s32[]{:S(2)}) async-start(), calls=%async_computation.1 | async-start | bytes 4718592 | tf_op jit(solution)/shard_map/all_gather | solution.py:28
  11.6 5.8 %copy-start = (bf16[2048,4096]{1,0:T(8,128)(2,1)S(1)}, bf16[2048,4096]{1,0:T(8,128)(2,1)}, u32[]{:S(2)}) copy-start(bf16[2048,4096]{1,0:T(8,128)(2,1)} %param.5) | copy-start | bytes 50331652
  112.5 2.0 copy-start.1
  115.7 22.7 %collective-permute-start.1 = (bf16[2048,128]{0,1:T(8,128)(2,1)S(1)}, bf16[2048,128]{0,1:T(8,128)(2,1)S(1)}, u32[]{:S(2)}, u32[]{:S(2)}) collective-permute-start(bf16[2048,128]{0,1:T(8,128)(2,1)S(1)} %get-tuple-element.7), channel_id=1, source_target_pairs={{0,1},{1,2},{2,3},{3,4},{4,5},{5,6},{6,7},{7,0},{8,9},{9,10},{10,1... | collective-permute-start | bytes 1572872 | tf_op jit(solution)/shard_map/ppermute | solution.py:40
  118.7 27.0 %collective-permute-start.2 = (bf16[2048,128]{0,1:T(8,128)(2,1)S(1)}, bf16[2048,128]{0,1:T(8,128)(2,1)S(1)}, u32[]{:S(2)}, u32[]{:S(2)}) collective-permute-start(bf16[2048,128]{0,1:T(8,128)(2,1)S(1)} %get-tuple-element.13), channel_id=1, source_target_pairs={{0,2},{1,3},{2,4},{3,5},{4,6},{5,7},{6,0},{7,1},{8,10},{9,11},{10,... | collective-permute-start | bytes 1572872 | tf_op jit(solution)/shard_map/ppermute | solution.py:40
  120.2 52.2 %collective-permute-start.3 = (bf16[2048,128]{0,1:T(8,128)(2,1)}, bf16[2048,128]{0,1:T(8,128)(2,1)}, u32[]{:S(2)}, u32[]{:S(2)}) collective-permute-start(bf16[2048,128]{0,1:T(8,128)(2,1)} %get-tuple-element.12), channel_id=1, source_target_pairs={{0,3},{1,4},{2,5},{3,6},{4,7},{5,0},{6,1},{7,2},{8,11},{9,12},{10,... | collective-permute-start | bytes 1572872 | tf_op jit(solution)/shard_map/ppermute | solution.py:40
  122.2 51.4 %collective-permute-start.4 = (bf16[2048,128]{0,1:T(8,128)(2,1)S(1)}, bf16[2048,128]{0,1:T(8,128)(2,1)}, u32[]{:S(2)}, u32[]{:S(2)}) collective-permute-start(bf16[2048,128]{0,1:T(8,128)(2,1)S(1)} %get-tuple-element.11), channel_id=1, source_target_pairs={{0,4},{1,5},{2,6},{3,7},{4,0},{5,1},{6,2},{7,3},{8,12},{9,13},{10,... | collective-permute-start | bytes 1572872 | tf_op jit(solution)/shard_map/ppermute | solution.py:40
  124.3 62.4 %collective-permute-start.5 = (bf16[2048,128]{0,1:T(8,128)(2,1)S(1)}, bf16[2048,128]{0,1:T(8,128)(2,1)}, u32[]{:S(2)}, u32[]{:S(2)}) collective-permute-start(bf16[2048,128]{0,1:T(8,128)(2,1)S(1)} %get-tuple-element.10), channel_id=1, source_target_pairs={{0,5},{1,6},{2,7},{3,0},{4,1},{5,2},{6,3},{7,4},{8,13},{9,14},{10,... | collective-permute-start | bytes 1572872 | tf_op jit(solution)/shard_map/ppermute | solution.py:40
  138.4 48.3 %collective-permute-start.6 = (bf16[2048,128]{0,1:T(8,128)(2,1)S(1)}, bf16[2048,128]{0,1:T(8,128)(2,1)}, u32[]{:S(2)}, u32[]{:S(2)}) collective-permute-start(bf16[2048,128]{0,1:T(8,128)(2,1)S(1)} %get-tuple-element.9), channel_id=1, source_target_pairs={{0,6},{1,7},{2,0},{3,1},{4,2},{5,3},{6,4},{7,5},{8,14},{9,15},{10,... | collective-permute-start | bytes 1572872 | tf_op jit(solution)/shard_map/ppermute | solution.py:40
  145.7 44.0 %collective-permute-start.7 = (bf16[2048,128]{0,1:T(8,128)(2,1)S(1)}, bf16[2048,128]{0,1:T(8,128)(2,1)}, u32[]{:S(2)}, u32[]{:S(2)}) collective-permute-start(bf16[2048,128]{0,1:T(8,128)(2,1)S(1)} %get-tuple-element.8), channel_id=1, source_target_pairs={{0,7},{1,0},{2,1},{3,2},{4,3},{5,4},{6,5},{7,6},{8,15},{9,8},{10,9... | collective-permute-start | bytes 1572872 | tf_op jit(solution)/shard_map/ppermute | solution.py:40
Sparse Core Ops, SparseCore 0:
  10.3 75.7 all-gather.5
  88.3 114.6 all-gather.3

commit v5 on v2

--- a/solution.py
+++ b/solution.py
@@ -14,6 +14,7 @@
 
 def make_local(n_row, n_col):
     ratio = n_row // n_col
+    assert ratio == 2
 
     perm = []
     for src_r in range(n_row):
@@ -22,10 +23,28 @@
             dst_r = h * n_col + o
             perm.append((src_r * n_col + o, dst_r * n_col + g))
 
+    def linear(r, c):
+        return r * n_col + c
+
+    spread_perms = []
+    for k in range(n_col):
+        pairs = []
+        for r in range(n_row):
+            for c in range(n_col):
+                b = (c + k) % n_col
+                pairs.append((linear(r, c), linear(ratio * b + r % ratio, r // ratio)))
+        spread_perms.append(pairs)
+    land_same = [(linear(ratio * b + h, j), linear(ratio * j + h, b))
+                 for b in range(n_col) for h in range(ratio) for j in range(n_col)]
+    land_other = [(linear(ratio * b + h, j), linear(ratio * j + 1 - h, b))
+                  for b in range(n_col) for h in range(ratio) for j in range(n_col)]
+
     def local(coeffs, intersection, coeff_mask, intersection_mask):
         masked_c = mask_blocks(coeffs, coeff_mask)
         rows, width = masked_c.shape
-        own_rows = lax.all_gather(masked_c, "col", axis=1, tiled=True)
+        me_row = lax.axis_index("row")
+        me_col = lax.axis_index("col")
+        half = me_row % ratio
         moved = lax.ppermute(masked_c, ("row", "col"), perm)
         gathered = lax.all_gather(moved, "row", axis=0, tiled=False)
         group_c = gathered.reshape(ratio, n_col, rows, width)
@@ -33,19 +52,24 @@
         pieces = jnp.einsum(
             "rhk,hokn->orn", masked_s, group_c, preferred_element_type=jnp.float32
         ).astype(jnp.bfloat16)
-        pieces = lax.all_to_all(pieces, "col", 0, 0, tiled=True)
-        summed = jnp.sum(pieces.astype(jnp.float32), axis=0)
+        summed = None
+        for k in range(n_col):
+            out = lax.dynamic_index_in_dim(pieces, (me_col + k) % n_col, 0, keepdims=False)
+            got = lax.ppermute(out, ("row", "col"), spread_perms[k]).astype(jnp.float32)
+            summed = got if summed is None else summed + got
         rounded = lax.reduce_precision(summed, exponent_bits=8, mantissa_bits=7)
         high = rounded.astype(jnp.bfloat16)
         low = (summed - rounded).astype(jnp.bfloat16)
         both = jnp.concatenate([high, low], axis=1)
-        partial = lax.dot_general(
-            own_rows, both, (((0,), (0,)), ((), ())), preferred_element_type=jnp.float32
-        )
-        partial = partial[:, :width] + partial[:, width:]
-        spread = partial.reshape(n_row, -1, width)
-        spread = lax.all_to_all(spread, "row", 0, 0, tiled=True)
-        return jnp.sum(spread, axis=0)
+        c_rows = lax.dynamic_index_in_dim(group_c, half, 0, keepdims=False)
+        partial = jnp.einsum("okn,km->onm", c_rows, both, preferred_element_type=jnp.float32)
+        partial = partial[:, :, :width] + partial[:, :, width:]
+        partial = lax.all_to_all(partial, "col", 0, 0, tiled=True)
+        total = jnp.sum(partial, axis=0).reshape(ratio, -1, width)
+        mine = lax.dynamic_index_in_dim(total, half, 0, keepdims=False)
+        theirs = lax.dynamic_index_in_dim(total, 1 - half, 0, keepdims=False)
+        return (lax.ppermute(mine, ("row", "col"), land_same)
+                + lax.ppermute(theirs, ("row", "col"), land_other))
 
     return local
 

time: 235 us -> 268 us (1.14)
  the two profiles are of different devices: /device:TPU:0 before, /device:TPU:24 now
where the time goes in v5:
time: 268 us; the launch traced here: 267 us
  waiting for transfers between devices  121 us (45%)
  starting transfers between devices  53.3 us (20%)
  local copies, waits for them, and re-layouts  36.2 us (14%)
  matrix products  29.9 us (11%)
  between operations  13.6 us (5%)
  other arithmetic  13.2 us (5%)
    ppermute x8, waiting for transfers between devices, local(): got = lax.ppermute(out, ('row', 'col'), spread_perms[k]).astype(jnp.float32)  74.6 us
    ppermute x8, starting transfers between devices, local(): got = lax.ppermute(out, ('row', 'col'), spread_perms[k]).astype(jnp.float32)  31.7 us
    mul x3, local copies, waits for them, and re-layouts, mask_blocks(): shaped * mask.astype(data.dtype)[:, None, :, None]  30.9 us
    dot_general x1, matrix products, local(): jnp.einsum('rhk,hokn->orn', masked_s, group_c, preferred_element_type=jnp...  26.4 us
    ppermute x1, waiting for transfers between devices, local(): moved = lax.ppermute(masked_c, ('row', 'col'), perm)  17.2 us
    all_gather x1, waiting for transfers between devices, local(): gathered = lax.all_gather(moved, 'row', axis=0, tiled=False)  13 us
    ppermute x1, starting transfers between devices, local(): lax.ppermute(mine, ('row', 'col'), land_same)  12.7 us
    all_to_all x1, waiting for transfers between devices, local(): partial = lax.all_to_all(partial, 'col', 0, 0, tiled=True)  9.09 us
  transfers between devices with their start and end apart: 13, of which 9 were waited for; matrix products, arithmetic and copies ran while one was open for 14% of the time, Pallas kernels for 0%

profile of v5, /device:TPU:24, one launch (start us, length us, event | category | flops | bytes accessed | tf_op | source)
XLA Modules:
  0.0 266.9 jit_solution(15922555313496828367)
XLA Ops:
  6.5 0.0 all-gather.3.cloned.1.call-start
  6.5 0.7 convert_bitcast_fusion
  7.2 0.1 broadcast_bitcast_fusion
  7.3 1.4 broadcast_multiply_fusion
  8.7 4.4 %collective-permute-start = (bf16[2048,128]{1,0:T(8,128)(2,1)S(1)}, bf16[2048,128]{1,0:T(8,128)(2,1)S(1)}, u32[]{:S(2)}, u32[]{:S(2)}) collective-permute-start(bf16[2048,128]{1,0:T(8,128)(2,1)S(1)} %broadcast_multiply_fusion), channel_id=1, source_target_pairs={{0,0},{1,8},{2,16},{3,24},{4,32},{5,40},{6,48},{7,56},{8,64},{9,72... | collective-permute-start | bytes 1572872 | tf_op jit(solution)/shard_map/ppermute | solution.py:48
  13.1 17.2 %collective-permute-done = bf16[2048,128]{1,0:T(8,128)(2,1)S(1)} collective-permute-done((bf16[2048,128]{1,0:T(8,128)(2,1)S(1)}, bf16[2048,128]{1,0:T(8,128)(2,1)S(1)}, u32[]{:S(2)}, u32[]{:S(2)}) %collective-permute-start) | collective-permute-done | bytes 524320 | tf_op jit(solution)/shard_map/ppermute | solution.py:48
  30.3 0.0 copy-start.1
  30.3 0.8 copy-done.1
  31.1 0.0 all-gather.3.cloned.1.call-update
  31.2 0.7 convert_element_type.41
  31.9 0.0 copy-start
  31.9 2.8 %mul.36 = bf16[16,128,32,128]{3,2,1,0:T(8,128)(2,1)S(1)} broadcast(bf16[16,32]{1,0:T(8,128)(2,1)S(1)} %convert_element_type.41), dimensions={0,2} | broadcast | bytes 16778240 | tf_op jit(solution)/shard_map/mul | solution.py:12
  34.8 2.9 %copy-done = bf16[2048,4096]{1,0:T(8,128)(2,1)S(1)} copy-done((bf16[2048,4096]{1,0:T(8,128)(2,1)S(1)}, bf16[2048,4096]{1,0:T(8,128)(2,1)}, u32[]{:S(2)}) %copy-start) | copy-done | bytes 16777240
  37.7 7.0 %bitcast_multiply_fusion = bf16[2048,4096]{1,0:T(8,128)(2,1)} fusion(bf16[2048,4096]{1,0:T(8,128)(2,1)S(1)} %copy-done, bf16[256,8,32,128]{3,2,1,0:T(8,128)(2,1)S(1)} %bitcast.57), kind=kLoop, calls=%fused_computation | loop fusion | flops 8388608 | bytes 50331648 | tf_op jit(solution)/shard_map/mul | solution.py:12
  44.7 28.0 %mul.39 = bf16[2048,2,2048]{2,1,0:T(2,128)(2,1)} reshape(bf16[2048,4096]{1,0:T(8,128)(2,1)} %bitcast_multiply_fusion) | data formatting | bytes 33554432 | tf_op jit(solution)/shard_map/mul | solution.py:12
  72.7 13.0 %all-gather.3.cloned.1.call-done = bf16[32768,128]{1,0:T(8,128)(2,1)} async-done(((bf16[2048,128]{1,0:T(8,128)(2,1)}), bf16[32768,128]{1,0:T(8,128)(2,1)}) %all-gather.3.cloned.1.call-update) | async-done | bytes 8388624 | tf_op jit(solution)/shard_map/all_gather | solution.py:49
  85.7 26.4 %bitcast_convert_fusion = bf16[8,128,2048]{2,1,0:T(8,128)(2,1)S(1)} fusion(bf16[2,8,2048,128]{3,2,1,0:T(8,128)(2,1)} %bitcast.60, bf16[2048,2,2048,1]{2,1,0,3:T(2,128)(2,1)} %bitcast.58), kind=kOutput, calls=%fused_computation.3 | convolution fusion | flops 17181966336 | bytes 29360128 | tf_op jit(solution)/shard_map/rhk,hokn->orn/dot_general | solution.py:52
  112.2 1.5 dynamic-slice_bitcast_fusion.7
  113.7 3.5 %collective-permute-start.8 = (bf16[2048,128]{0,1:T(8,128)(2,1)S(1)}, bf16[2048,128]{0,1:T(8,128)(2,1)S(1)}, u32[]{:S(2)}, u32[]{:S(2)}) collective-permute-start(bf16[2048,128]{0,1:T(8,128)(2,1)S(1)} %get-tuple-element.8), channel_id=1, source_target_pairs={{0,112},{1,0},{2,16},{3,32},{4,48},{5,64},{6,80},{7,96},{8,120},{9... | collective-permute-start | bytes 1572872 | tf_op jit(solution)/shard_map/ppermute | solution.py:58
  117.2 3.2 %collective-permute-start.7 = (bf16[2048,128]{0,1:T(8,128)(2,1)S(1)}, bf16[2048,128]{0,1:T(8,128)(2,1)S(1)}, u32[]{:S(2)}, u32[]{:S(2)}) collective-permute-start(bf16[2048,128]{0,1:T(8,128)(2,1)S(1)} %get-tuple-element.9), channel_id=1, source_target_pairs={{0,96},{1,112},{2,0},{3,16},{4,32},{5,48},{6,64},{7,80},{8,104},{9... | collective-permute-start | bytes 1572872 | tf_op jit(solution)/shard_map/ppermute | solution.py:58
  120.4 2.3 collective-permute-start.6
  122.7 0.5 collective-permute-start.5
  123.2 4.4 %collective-permute-start.4 = (bf16[2048,128]{0,1:T(8,128)(2,1)}, bf16[2048,128]{0,1:T(8,128)(2,1)S(1)}, u32[]{:S(2)}, u32[]{:S(2)}) collective-permute-start(bf16[2048,128]{0,1:T(8,128)(2,1)} %get-tuple-element.12), channel_id=1, source_target_pairs={{0,48},{1,64},{2,80},{3,96},{4,112},{5,0},{6,16},{7,32},{8,56},{9,... | collective-permute-start | bytes 1572872 | tf_op jit(solution)/shard_map/ppermute | solution.py:58
  127.6 18.2 %collective-permute-done.8 = bf16[2048,128]{0,1:T(8,128)(2,1)S(1)} collective-permute-done((bf16[2048,128]{0,1:T(8,128)(2,1)S(1)}, bf16[2048,128]{0,1:T(8,128)(2,1)S(1)}, u32[]{:S(2)}, u32[]{:S(2)}) %collective-permute-start.8) | collective-permute-done | bytes 524320 | tf_op jit(solution)/shard_map/ppermute | solution.py:58
  145.8 5.1 %collective-permute-start.3 = (bf16[2048,128]{0,1:T(8,128)(2,1)}, bf16[2048,128]{0,1:T(8,128)(2,1)S(1)}, u32[]{:S(2)}, u32[]{:S(2)}) collective-permute-start(bf16[2048,128]{0,1:T(8,128)(2,1)} %get-tuple-element.13), channel_id=1, source_target_pairs={{0,32},{1,48},{2,64},{3,80},{4,96},{5,112},{6,0},{7,16},{8,40},{9,... | collective-permute-start | bytes 1572872 | tf_op jit(solution)/shard_map/ppermute | solution.py:58
  150.8 16.2 %collective-permute-done.7 = bf16[2048,128]{0,1:T(8,128)(2,1)S(1)} collective-permute-done((bf16[2048,128]{0,1:T(8,128)(2,1)S(1)}, bf16[2048,128]{0,1:T(8,128)(2,1)S(1)}, u32[]{:S(2)}, u32[]{:S(2)}) %collective-permute-start.7) | collective-permute-done | bytes 524320 | tf_op jit(solution)/shard_map/ppermute | solution.py:58
  167.1 10.6 %collective-permute-start.2 = (bf16[2048,128]{0,1:T(8,128)(2,1)}, bf16[2048,128]{0,1:T(8,128)(2,1)}, u32[]{:S(2)}, u32[]{:S(2)}) collective-permute-start(bf16[2048,128]{0,1:T(8,128)(2,1)} %get-tuple-element.14), channel_id=1, source_target_pairs={{0,16},{1,32},{2,48},{3,64},{4,80},{5,96},{6,112},{7,0},{8,24},{9,... | collective-permute-start | bytes 1572872 | tf_op jit(solution)/shard_map/ppermute | solution.py:58
  177.7 0.0 collective-permute-done.6
  177.7 2.1 collective-permute-start.1
  179.8 0.0 collective-permute-done.5
  179.8 0.0 collective-permute-done.4
  179.8 0.0 collective-permute-done.3
  179.8 22.3 %collective-permute-done.2 = bf16[2048,128]{0,1:T(8,128)(2,1)} collective-permute-done((bf16[2048,128]{0,1:T(8,128)(2,1)}, bf16[2048,128]{0,1:T(8,128)(2,1)}, u32[]{:S(2)}, u32[]{:S(2)}) %collective-permute-start.2) | collective-permute-done | bytes 524320 | tf_op jit(solution)/shard_map/ppermute | solution.py:58
  202.1 17.9 %collective-permute-done.1 = bf16[2048,128]{0,1:T(8,128)(2,1)} collective-permute-done((bf16[2048,128]{0,1:T(8,128)(2,1)}, bf16[2048,128]{0,1:T(8,128)(2,1)}, u32[]{:S(2)}, u32[]{:S(2)}) %collective-permute-start.1) | collective-permute-done | bytes 524320 | tf_op jit(solution)/shard_map/ppermute | solution.py:58
  220.0 1.9 reduce-precision_convert_fusion
  221.9 0.1 fusion.7
  222.0 3.5 %fusion.4 = f32[8,128,256]{2,1,0:T(8,128)S(1)} fusion(bf16[2,8,2048,128]{3,2,1,0:T(8,128)(2,1)} %bitcast.61, s32[]{:T(128)S(6)} %select_n.74, bf16[2048,128]{0,1:T(8,128)(2,1)S(1)} %fusion.7, bf16[2048,128]{0,1:T(8,128)(2,1)S(1)} %get-tuple-element.5), kind=kOutput, calls=%fused_computation.4 | convolution fusion | flops 1075838976 | bytes 6291460 | tf_op jit(solution)/shard_map/okn,km->onm/dot_general | solution.py:65
  225.5 0.9 slice_add_fusion
  226.4 4.5 %all-to-all-start = ((f32[8,128,128]{2,1,0:T(8,128)}), f32[8,128,128]{2,1,0:T(8,128)S(1)}, u32[]{:S(2)}, u32[]{:S(2)}) async-start(f32[8,128,128]{2,1,0:T(8,128)} %slice_add_fusion), calls=%async_computation | async-start | bytes 1048576 | tf_op jit(solution)/shard_map/all_to_all | solution.py:67
  230.9 9.1 %all-to-all-done = f32[8,128,128]{2,1,0:T(8,128)S(1)} async-done(((f32[8,128,128]{2,1,0:T(8,128)}), f32[8,128,128]{2,1,0:T(8,128)S(1)}, u32[]{:S(2)}, u32[]{:S(2)}) %all-to-all-start) | async-done | bytes 524320 | tf_op jit(solution)/shard_map/all_to_all | solution.py:67
  240.0 12.7 %collective-permute-start.9 = (f32[64,128]{1,0:T(8,128)S(1)}, f32[64,128]{1,0:T(8,128)S(1)}, u32[]{:S(2)}, u32[]{:S(2)}) collective-permute-start(f32[64,128]{1,0:T(8,128)S(1)} %get-tuple-element.16), channel_id=1, source_target_pairs={{0,0},{1,16},{2,32},{3,48},{4,64},{5,80},{6,96},{7,112},{8,8},{9,2... | collective-permute-start | bytes 98312 | tf_op jit(solution)/shard_map/ppermute | solution.py:71
  252.7 0.1 collective-permute-start.10
  252.8 1.8 collective-permute-done.9
  254.6 4.9 %collective-permute-done.10 = f32[64,128]{1,0:T(8,128)S(1)} collective-permute-done((f32[64,128]{1,0:T(8,128)S(1)}, f32[64,128]{1,0:T(8,128)S(1)}, u32[]{:S(2)}, u32[]{:S(2)}) %collective-permute-start.10) | collective-permute-done | bytes 32800 | tf_op jit(solution)/shard_map/ppermute | solution.py:72
  259.4 0.6 add.145
  (2 shorter events, 0.0 us)
Async XLA Ops:
  6.5 79.2 %all-gather.3.cloned.1.call-start = ((), (), s32[]{:S(2)}) async-start(), calls=%async_computation.1 | async-start | bytes 8912896 | tf_op jit(solution)/shard_map/all_gather | solution.py:49
  8.7 21.7 %collective-permute-start = (bf16[2048,128]{1,0:T(8,128)(2,1)S(1)}, bf16[2048,128]{1,0:T(8,128)(2,1)S(1)}, u32[]{:S(2)}, u32[]{:S(2)}) collective-permute-start(bf16[2048,128]{1,0:T(8,128)(2,1)S(1)} %broadcast_multiply_fusion), channel_id=1, source_target_pairs={{0,0},{1,8},{2,16},{3,24},{4,32},{5,40},{6,48},{7,56},{8,64},{9,72... | collective-permute-start | bytes 1572872 | tf_op jit(solution)/shard_map/ppermute | solution.py:48
  30.3 0.8 copy-start.1
  31.9 5.8 %copy-start = (bf16[2048,4096]{1,0:T(8,128)(2,1)S(1)}, bf16[2048,4096]{1,0:T(8,128)(2,1)}, u32[]{:S(2)}) copy-start(bf16[2048,4096]{1,0:T(8,128)(2,1)} %param.5) | copy-start | bytes 50331652
  113.7 32.1 %collective-permute-start.8 = (bf16[2048,128]{0,1:T(8,128)(2,1)S(1)}, bf16[2048,128]{0,1:T(8,128)(2,1)S(1)}, u32[]{:S(2)}, u32[]{:S(2)}) collective-permute-start(bf16[2048,128]{0,1:T(8,128)(2,1)S(1)} %get-tuple-element.8), channel_id=1, source_target_pairs={{0,112},{1,0},{2,16},{3,32},{4,48},{5,64},{6,80},{7,96},{8,120},{9... | collective-permute-start | bytes 1572872 | tf_op jit(solution)/shard_map/ppermute | solution.py:58
  117.2 49.9 %collective-permute-start.7 = (bf16[2048,128]{0,1:T(8,128)(2,1)S(1)}, bf16[2048,128]{0,1:T(8,128)(2,1)S(1)}, u32[]{:S(2)}, u32[]{:S(2)}) collective-permute-start(bf16[2048,128]{0,1:T(8,128)(2,1)S(1)} %get-tuple-element.9), channel_id=1, source_target_pairs={{0,96},{1,112},{2,0},{3,16},{4,32},{5,48},{6,64},{7,80},{8,104},{9... | collective-permute-start | bytes 1572872 | tf_op jit(solution)/shard_map/ppermute | solution.py:58
  120.4 57.2 %collective-permute-start.6 = (bf16[2048,128]{0,1:T(8,128)(2,1)S(1)}, bf16[2048,128]{0,1:T(8,128)(2,1)S(1)}, u32[]{:S(2)}, u32[]{:S(2)}) collective-permute-start(bf16[2048,128]{0,1:T(8,128)(2,1)S(1)} %get-tuple-element.10), channel_id=1, source_target_pairs={{0,80},{1,96},{2,112},{3,0},{4,16},{5,32},{6,48},{7,64},{8,88},{9,... | collective-permute-start | bytes 1572872 | tf_op jit(solution)/shard_map/ppermute | solution.py:58
  122.7 57.1 %collective-permute-start.5 = (bf16[2048,128]{0,1:T(8,128)(2,1)}, bf16[2048,128]{0,1:T(8,128)(2,1)S(1)}, u32[]{:S(2)}, u32[]{:S(2)}) collective-permute-start(bf16[2048,128]{0,1:T(8,128)(2,1)} %get-tuple-element.11), channel_id=1, source_target_pairs={{0,64},{1,80},{2,96},{3,112},{4,0},{5,16},{6,32},{7,48},{8,72},{9,... | collective-permute-start | bytes 1572872 | tf_op jit(solution)/shard_map/ppermute | solution.py:58
  123.2 56.6 %collective-permute-start.4 = (bf16[2048,128]{0,1:T(8,128)(2,1)}, bf16[2048,128]{0,1:T(8,128)(2,1)S(1)}, u32[]{:S(2)}, u32[]{:S(2)}) collective-permute-start(bf16[2048,128]{0,1:T(8,128)(2,1)} %get-tuple-element.12), channel_id=1, source_target_pairs={{0,48},{1,64},{2,80},{3,96},{4,112},{5,0},{6,16},{7,32},{8,56},{9,... | collective-permute-start | bytes 1572872 | tf_op jit(solution)/shard_map/ppermute | solution.py:58
  145.8 34.0 %collective-permute-start.3 = (bf16[2048,128]{0,1:T(8,128)(2,1)}, bf16[2048,128]{0,1:T(8,128)(2,1)S(1)}, u32[]{:S(2)}, u32[]{:S(2)}) collective-permute-start(bf16[2048,128]{0,1:T(8,128)(2,1)} %get-tuple-element.13), channel_id=1, source_target_pairs={{0,32},{1,48},{2,64},{3,80},{4,96},{5,112},{6,0},{7,16},{8,40},{9,... | collective-permute-start | bytes 1572872 | tf_op jit(solution)/shard_map/ppermute | solution.py:58
  167.1 35.0 %collective-permute-start.2 = (bf16[2048,128]{0,1:T(8,128)(2,1)}, bf16[2048,128]{0,1:T(8,128)(2,1)}, u32[]{:S(2)}, u32[]{:S(2)}) collective-permute-start(bf16[2048,128]{0,1:T(8,128)(2,1)} %get-tuple-element.14), channel_id=1, source_target_pairs={{0,16},{1,32},{2,48},{3,64},{4,80},{5,96},{6,112},{7,0},{8,24},{9,... | collective-permute-start | bytes 1572872 | tf_op jit(solution)/shard_map/ppermute | solution.py:58
  177.7 42.3 %collective-permute-start.1 = (bf16[2048,128]{0,1:T(8,128)(2,1)}, bf16[2048,128]{0,1:T(8,128)(2,1)}, u32[]{:S(2)}, u32[]{:S(2)}) collective-permute-start(bf16[2048,128]{0,1:T(8,128)(2,1)} %get-tuple-element.7), channel_id=1, source_target_pairs={{0,0},{1,16},{2,32},{3,48},{4,64},{5,80},{6,96},{7,112},{8,8},{9,2... | collective-permute-start | bytes 1572872 | tf_op jit(solution)/shard_map/ppermute | solution.py:58
  226.4 13.6 %all-to-all-start = ((f32[8,128,128]{2,1,0:T(8,128)}), f32[8,128,128]{2,1,0:T(8,128)S(1)}, u32[]{:S(2)}, u32[]{:S(2)}) async-start(f32[8,128,128]{2,1,0:T(8,128)} %slice_add_fusion), calls=%async_computation | async-start | bytes 1048576 | tf_op jit(solution)/shard_map/all_to_all | solution.py:67
  240.0 14.5 %collective-permute-start.9 = (f32[64,128]{1,0:T(8,128)S(1)}, f32[64,128]{1,0:T(8,128)S(1)}, u32[]{:S(2)}, u32[]{:S(2)}) collective-permute-start(f32[64,128]{1,0:T(8,128)S(1)} %get-tuple-element.16), channel_id=1, source_target_pairs={{0,0},{1,16},{2,32},{3,48},{4,64},{5,80},{6,96},{7,112},{8,8},{9,2... | collective-permute-start | bytes 98312 | tf_op jit(solution)/shard_map/ppermute | solution.py:71
  252.7 6.7 %collective-permute-start.10 = (f32[64,128]{1,0:T(8,128)S(1)}, f32[64,128]{1,0:T(8,128)S(1)}, u32[]{:S(2)}, u32[]{:S(2)}) collective-permute-start(f32[64,128]{1,0:T(8,128)S(1)} %get-tuple-element.15), channel_id=1, source_target_pairs={{0,8},{1,24},{2,40},{3,56},{4,72},{5,88},{6,104},{7,120},{8,0},{9,... | collective-permute-start | bytes 98312 | tf_op jit(solution)/shard_map/ppermute | solution.py:72
Sparse Core Ops, SparseCore 0:
  31.3 54.4 all-gather.2

commit v6 on v4

--- a/solution.py
+++ b/solution.py
@@ -27,12 +27,20 @@
         rows, width = masked_c.shape
         own_rows = lax.all_gather(masked_c, "col", axis=1, tiled=True)
         moved = lax.ppermute(masked_c, ("row", "col"), perm)
-        gathered = lax.all_gather(moved, "row", axis=0, tiled=False)
-        group_c = gathered.reshape(ratio, n_col, rows, width)
-        masked_s = mask_blocks(intersection, intersection_mask).reshape(rows, ratio, rows)
-        pieces = jnp.einsum(
-            "rhk,hokn->orn", masked_s, group_c, preferred_element_type=jnp.float32
-        ).astype(jnp.bfloat16)
+        half_rows = rows // 2
+        gathered = [
+            lax.all_gather(moved[j * half_rows:(j + 1) * half_rows], "row", axis=0, tiled=False)
+            for j in range(2)
+        ]
+        masked_s = mask_blocks(intersection, intersection_mask).reshape(rows, ratio, 2, half_rows)
+        pieces = None
+        for j in range(2):
+            group_c = gathered[j].reshape(ratio, n_col, half_rows, width)
+            part = jnp.einsum(
+                "rhk,hokn->orn", masked_s[:, :, j], group_c, preferred_element_type=jnp.float32
+            )
+            pieces = part if pieces is None else pieces + part
+        pieces = pieces.astype(jnp.bfloat16)
         me = lax.axis_index("col")
         summed = lax.dynamic_index_in_dim(pieces, me, 0, keepdims=False).astype(jnp.float32)
         for k in range(1, n_col):

time: 233 us -> 286 us (1.23)
  local copies, waits for them, and re-layouts: 37.6 us -> 104 us
  waiting for transfers between devices: 78.7 us -> 37.1 us
  other arithmetic: 13 us -> 26.4 us
  starting transfers between devices: 41.3 us -> 54.2 us
    all_gather x1 -> x2, waiting for transfers between devices: 33.9 us -> 0.01 us  [local(): lax.all_gather(moved[j * half_rows:(j + 1) * half_rows], 'row', axis=0, t...]
    mul x3 -> x4, local copies, waits for them, and re-layouts: 30.7 us -> 54.3 us  [mask_blocks(): shaped * mask.astype(data.dtype)[:, None, :, None]]
    reshape x0 -> x1, local copies, waits for them, and re-layouts: none -> 22.8 us  [mask_blocks(): shaped = data.reshape(rows // BLK, BLK, cols // BLK, BLK)]
    unnamed x8 -> x5, local copies, waits for them, and re-layouts: 5.69 us -> 24.6 us
    mul x3, other arithmetic: 9.03 us -> 22.4 us  [mask_blocks(): shaped * mask.astype(data.dtype)[:, None, :, None]]
    ppermute x7, starting transfers between devices: 40.6 us -> 53.4 us  [local(): got = lax.ppermute(out, 'col', [(c, (c + k) % n_col) for c in range(n_col)])]
    all_gather x1, waiting for transfers between devices: 10.7 us -> 0.02 us  [local(): own_rows = lax.all_gather(masked_c, 'col', axis=1, tiled=True)]
    dot_general x1 -> x2, matrix products: 26.4 us -> 28.8 us  [local(): jnp.einsum('rhk,hokn->orn', masked_s[:, :, j], group_c, preferred_element...]
  transfers between devices with their start and end apart: 10 -> 11, of which waited for: 7 -> 5; matrix products, arithmetic and copies ran while one was open for 30% -> 55% of each run, Pallas kernels for 0% -> 0%
where the time goes in v6:
time: 286 us; the launch traced here: 281 us
  local copies, waits for them, and re-layouts  104 us (36%)
  starting transfers between devices  54.2 us (19%)
  waiting for transfers between devices  37.1 us (13%)
  matrix products  32.3 us (11%)
  other arithmetic  26.4 us (9%)
  blocking collectives  13.9 us (5%)
  between operations  13.3 us (5%)
    mul x4, local copies, waits for them, and re-layouts, mask_blocks(): shaped * mask.astype(data.dtype)[:, None, :, None]  54.3 us
    ppermute x7, starting transfers between devices, local(): got = lax.ppermute(out, 'col', [(c, (c + k) % n_col) for c in range(n_col)])  53.4 us
    ppermute x7, waiting for transfers between devices, local(): got = lax.ppermute(out, 'col', [(c, (c + k) % n_col) for c in range(n_col)])  35.7 us
    dot_general x2, matrix products, local(): jnp.einsum('rhk,hokn->orn', masked_s[:, :, j], group_c, preferred_element...  28.8 us
    unnamed x5, local copies, waits for them, and re-layouts  24.6 us
    reshape x1, local copies, waits for them, and re-layouts, mask_blocks(): shaped = data.reshape(rows // BLK, BLK, cols // BLK, BLK)  22.8 us
    mul x3, other arithmetic, mask_blocks(): shaped * mask.astype(data.dtype)[:, None, :, None]  22.4 us
    all_to_all x1, blocking collectives, local(): spread = lax.all_to_all(spread, 'row', 0, 0, tiled=True)  13.9 us
  transfers between devices with their start and end apart: 11, of which 5 were waited for; matrix products, arithmetic and copies ran while one was open for 55% of the time, Pallas kernels for 0%

profile of v6, /device:TPU:0, one launch (start us, length us, event | category | flops | bytes accessed | tf_op | source)
XLA Modules:
  0.0 280.8 jit_solution(14309194191084121939)
XLA Ops:
  6.5 0.0 all-gather.8.cloned.1.call-start
  6.5 0.7 convert_bitcast_fusion
  7.2 0.1 broadcast_bitcast_fusion
  7.3 1.4 broadcast_multiply_fusion
  8.7 0.0 copy-start.1
  8.7 0.7 collective-permute-start
  9.4 0.0 collective-permute-done
  9.4 0.8 fusion.16
  10.2 0.0 all-gather.8.cloned.1.call-update
  10.2 0.0 all-gather.10.cloned.1.call-start
  10.3 0.7 all-gather.10.cloned.1.call-update
  11.0 0.0 all-gather.6.cloned.1.call-start
  11.0 0.0 copy-done.1
  11.0 0.7 all-gather.6.cloned.1.call-update
  11.8 0.7 convert_element_type.47
  12.5 0.1 copy.6
  12.6 6.2 %mul.33 = bf16[16,128,32,128]{1,0,3,2:T(8,128)(2,1)} broadcast(bf16[16,32]{0,1:T(8,128)(2,1)S(1)} %copy.6), dimensions={0,2} | broadcast | bytes 16778240 | tf_op jit(solution)/shard_map/mul | solution.py:12
  18.8 25.3 %mul.34 = bf16[2048,2,2,1024]{0,3,2,1:T(8,128)(2,1)} reshape(bf16[16,128,32,128]{1,0,3,2:T(8,128)(2,1)} %mul.33) | data formatting | bytes 33554432 | tf_op jit(solution)/shard_map/mul | solution.py:12
  44.1 22.7 %copy.8 = bf16[2048,2,2,1024]{3,0,1,2:T(8,128)(2,1)} copy(bf16[2048,2,2,1024]{0,3,2,1:T(8,128)(2,1)} %mul.34) | data formatting | bytes 33554432 | tf_op jit(solution)/shard_map/mul | solution.py:12
  66.8 22.7 %copy.5 = bf16[2048,4096]{0,1:T(8,128)(2,1)} copy(bf16[2048,4096]{1,0:T(8,128)(2,1)} %param.5) | data formatting | bytes 33554432 | tf_op args[1]
  89.5 22.8 %copy.7 = bf16[2048,2,2,1024]{3,0,1,2:T(8,128)(2,1)} copy(bf16[2048,2,2,1024]{0,3,2,1:T(8,128)(2,1)} %bitcast.80) | data formatting | bytes 33554432 | tf_op jit(solution)/shard_map/reshape | solution.py:11
  112.2 20.3 %mul.35 = bf16[2048,2,2,1024]{3,0,1,2:T(8,128)(2,1)} multiply(bf16[2048,2,2,1024]{3,0,1,2:T(8,128)(2,1)} %copy.7, bf16[2048,2,2,1024]{3,0,1,2:T(8,128)(2,1)} %copy.8) | non-fusion elementwise | flops 8388608 | bytes 50331648 | tf_op jit(solution)/shard_map/mul | solution.py:12
  132.6 14.6 %fusion.1 = f32[8,128,2048,1]{2,1,0,3:T(8,128)} fusion(bf16[2,8,1024,128]{3,2,1,0:T(8,128)(2,1)} %bitcast.82, bf16[2048,2,2,1024]{3,0,1,2:T(8,128)(2,1)} %mul.35), kind=kOutput, calls=%fused_computation.3 | convolution fusion | flops 8589934592 | bytes 20971520 | tf_op jit(solution)/shard_map/rhk,hokn->orn/dot_general | solution.py:39
  147.2 14.2 %fusion.2 = bf16[8,128,2048]{2,1,0:T(8,128)(2,1)S(1)} fusion(f32[8,128,2048,1]{2,1,0,3:T(8,128)} %fusion.1, bf16[2,8,1024,128]{3,2,1,0:T(8,128)(2,1)} %bitcast.83, bf16[2048,2,2,1024]{3,0,1,2:T(8,128)(2,1)} %mul.35), kind=kOutput, calls=%fused_computation.5 | convolution fusion | flops 8594128896 | bytes 25165824 | tf_op jit(solution)/shard_map/rhk,hokn->orn/dot_general | solution.py:39
  161.3 0.0 copy-start
  161.4 1.9 copy-done
  163.3 1.2 dynamic-slice_bitcast_fusion.6
  164.5 14.0 %collective-permute-start.1 = (bf16[2048,128]{0,1:T(8,128)(2,1)S(1)}, bf16[2048,128]{0,1:T(8,128)(2,1)S(1)}, u32[]{:S(2)}, u32[]{:S(2)}) collective-permute-start(bf16[2048,128]{0,1:T(8,128)(2,1)S(1)} %get-tuple-element.7), channel_id=1, source_target_pairs={{0,1},{1,2},{2,3},{3,4},{4,5},{5,6},{6,7},{7,0},{8,9},{9,10},{10,1... | collective-permute-start | bytes 1572872 | tf_op jit(solution)/shard_map/ppermute | solution.py:48
  178.5 6.6 %collective-permute-start.2 = (bf16[2048,128]{0,1:T(8,128)(2,1)S(1)}, bf16[2048,128]{0,1:T(8,128)(2,1)S(1)}, u32[]{:S(2)}, u32[]{:S(2)}) collective-permute-start(bf16[2048,128]{0,1:T(8,128)(2,1)S(1)} %get-tuple-element.13), channel_id=1, source_target_pairs={{0,2},{1,3},{2,4},{3,5},{4,6},{5,7},{6,0},{7,1},{8,10},{9,11},{10,... | collective-permute-start | bytes 1572872 | tf_op jit(solution)/shard_map/ppermute | solution.py:48
  185.0 7.4 %collective-permute-start.3 = (bf16[2048,128]{0,1:T(8,128)(2,1)}, bf16[2048,128]{0,1:T(8,128)(2,1)}, u32[]{:S(2)}, u32[]{:S(2)}) collective-permute-start(bf16[2048,128]{0,1:T(8,128)(2,1)} %get-tuple-element.12), channel_id=1, source_target_pairs={{0,3},{1,4},{2,5},{3,6},{4,7},{5,0},{6,1},{7,2},{8,11},{9,12},{10,... | collective-permute-start | bytes 1572872 | tf_op jit(solution)/shard_map/ppermute | solution.py:48
  192.4 2.3 collective-permute-start.4
  194.7 5.9 %collective-permute-start.5 = (bf16[2048,128]{0,1:T(8,128)(2,1)S(1)}, bf16[2048,128]{0,1:T(8,128)(2,1)}, u32[]{:S(2)}, u32[]{:S(2)}) collective-permute-start(bf16[2048,128]{0,1:T(8,128)(2,1)S(1)} %get-tuple-element.10), channel_id=1, source_target_pairs={{0,5},{1,6},{2,7},{3,0},{4,1},{5,2},{6,3},{7,4},{8,13},{9,14},{10,... | collective-permute-start | bytes 1572872 | tf_op jit(solution)/shard_map/ppermute | solution.py:48
  200.7 4.8 %collective-permute-done.1 = bf16[2048,128]{0,1:T(8,128)(2,1)S(1)} collective-permute-done((bf16[2048,128]{0,1:T(8,128)(2,1)S(1)}, bf16[2048,128]{0,1:T(8,128)(2,1)S(1)}, u32[]{:S(2)}, u32[]{:S(2)}) %collective-permute-start.1) | collective-permute-done | bytes 524320 | tf_op jit(solution)/shard_map/ppermute | solution.py:48
  205.5 6.9 %collective-permute-start.6 = (bf16[2048,128]{0,1:T(8,128)(2,1)S(1)}, bf16[2048,128]{0,1:T(8,128)(2,1)}, u32[]{:S(2)}, u32[]{:S(2)}) collective-permute-start(bf16[2048,128]{0,1:T(8,128)(2,1)S(1)} %get-tuple-element.9), channel_id=1, source_target_pairs={{0,6},{1,7},{2,0},{3,1},{4,2},{5,3},{6,4},{7,5},{8,14},{9,15},{10,... | collective-permute-start | bytes 1572872 | tf_op jit(solution)/shard_map/ppermute | solution.py:48
  212.4 0.0 collective-permute-done.2
  212.4 10.3 %collective-permute-start.7 = (bf16[2048,128]{0,1:T(8,128)(2,1)S(1)}, bf16[2048,128]{0,1:T(8,128)(2,1)}, u32[]{:S(2)}, u32[]{:S(2)}) collective-permute-start(bf16[2048,128]{0,1:T(8,128)(2,1)S(1)} %get-tuple-element.8), channel_id=1, source_target_pairs={{0,7},{1,0},{2,1},{3,2},{4,3},{5,4},{6,5},{7,6},{8,15},{9,8},{10,9... | collective-permute-start | bytes 1572872 | tf_op jit(solution)/shard_map/ppermute | solution.py:48
  222.7 16.3 %collective-permute-done.3 = bf16[2048,128]{0,1:T(8,128)(2,1)} collective-permute-done((bf16[2048,128]{0,1:T(8,128)(2,1)}, bf16[2048,128]{0,1:T(8,128)(2,1)}, u32[]{:S(2)}, u32[]{:S(2)}) %collective-permute-start.3) | collective-permute-done | bytes 524320 | tf_op jit(solution)/shard_map/ppermute | solution.py:48
  239.0 2.1 collective-permute-done.4
  241.1 5.6 %collective-permute-done.5 = bf16[2048,128]{0,1:T(8,128)(2,1)} collective-permute-done((bf16[2048,128]{0,1:T(8,128)(2,1)S(1)}, bf16[2048,128]{0,1:T(8,128)(2,1)}, u32[]{:S(2)}, u32[]{:S(2)}) %collective-permute-start.5) | collective-permute-done | bytes 524320 | tf_op jit(solution)/shard_map/ppermute | solution.py:48
  246.7 0.0 collective-permute-done.6
  246.7 6.9 %collective-permute-done.7 = bf16[2048,128]{0,1:T(8,128)(2,1)} collective-permute-done((bf16[2048,128]{0,1:T(8,128)(2,1)S(1)}, bf16[2048,128]{0,1:T(8,128)(2,1)}, u32[]{:S(2)}, u32[]{:S(2)}) %collective-permute-start.7) | collective-permute-done | bytes 524320 | tf_op jit(solution)/shard_map/ppermute | solution.py:48
  253.6 2.5 reduce-precision_convert_fusion
  256.1 0.1 fusion.3
  256.2 0.0 all-gather.6.cloned.1.call-done
  256.2 3.5 %fusion.4 = f32[1024,256]{1,0:T(8,128)S(1)} fusion(bf16[2048,1024]{1,0:T(8,128)(2,1)} %all-gather.6.cloned.1.call-done, bf16[2048,128]{0,1:T(8,128)(2,1)S(1)} %fusion.3, bf16[2048,128]{0,1:T(8,128)(2,1)S(1)} %get-tuple-element.5), kind=kOutput, calls=%fused_computation.9 | convolution fusion | flops 1075838976 | bytes 6291456 | tf_op jit(solution)/shard_map/dot_general | solution.py:54
  259.8 0.1 slice_add_fusion
  259.8 13.9 %all_to_all.5 = f32[16,64,128]{2,1,0:T(8,128)S(1)} all-to-all(f32[16,64,128]{2,1,0:T(8,128)S(1)} %bitcast.81), channel_id=1, replica_groups=mesh['row'=16,'col'=8] {'row'}, dimensions={0} | all-to-all | bytes 1048576 | tf_op jit(solution)/shard_map/all_to_all | solution.py:59
  273.7 0.6 reduce_sum.9
  (2 shorter events, 0.0 us)
Async XLA Ops:
  6.5 126.0 %all-gather.8.cloned.1.call-start = ((), (), s32[]{:S(2)}) async-start(), calls=%async_computation.2 | async-start | bytes 4456448 | tf_op jit(solution)/shard_map/all_gather | solution.py:32
  8.7 2.4 copy-start.1
  8.7 0.7 collective-permute-start
  10.2 136.9 %all-gather.10.cloned.1.call-start = ((), (), s32[]{:S(2)}) async-start(), calls=%async_computation.3 | async-start | bytes 4456448 | tf_op jit(solution)/shard_map/all_gather | solution.py:32
  11.0 245.3 %all-gather.6.cloned.1.call-start = ((), (), s32[]{:S(2)}) async-start(), calls=%async_computation.1 | async-start | bytes 4718592 | tf_op jit(solution)/shard_map/all_gather | solution.py:28
  161.3 2.0 copy-start
  164.5 41.0 %collective-permute-start.1 = (bf16[2048,128]{0,1:T(8,128)(2,1)S(1)}, bf16[2048,128]{0,1:T(8,128)(2,1)S(1)}, u32[]{:S(2)}, u32[]{:S(2)}) collective-permute-start(bf16[2048,128]{0,1:T(8,128)(2,1)S(1)} %get-tuple-element.7), channel_id=1, source_target_pairs={{0,1},{1,2},{2,3},{3,4},{4,5},{5,6},{6,7},{7,0},{8,9},{9,10},{10,1... | collective-permute-start | bytes 1572872 | tf_op jit(solution)/shard_map/ppermute | solution.py:48
  178.5 34.0 %collective-permute-start.2 = (bf16[2048,128]{0,1:T(8,128)(2,1)S(1)}, bf16[2048,128]{0,1:T(8,128)(2,1)S(1)}, u32[]{:S(2)}, u32[]{:S(2)}) collective-permute-start(bf16[2048,128]{0,1:T(8,128)(2,1)S(1)} %get-tuple-element.13), channel_id=1, source_target_pairs={{0,2},{1,3},{2,4},{3,5},{4,6},{5,7},{6,0},{7,1},{8,10},{9,11},{10,... | collective-permute-start | bytes 1572872 | tf_op jit(solution)/shard_map/ppermute | solution.py:48
  185.0 54.0 %collective-permute-start.3 = (bf16[2048,128]{0,1:T(8,128)(2,1)}, bf16[2048,128]{0,1:T(8,128)(2,1)}, u32[]{:S(2)}, u32[]{:S(2)}) collective-permute-start(bf16[2048,128]{0,1:T(8,128)(2,1)} %get-tuple-element.12), channel_id=1, source_target_pairs={{0,3},{1,4},{2,5},{3,6},{4,7},{5,0},{6,1},{7,2},{8,11},{9,12},{10,... | collective-permute-start | bytes 1572872 | tf_op jit(solution)/shard_map/ppermute | solution.py:48
  192.4 48.7 %collective-permute-start.4 = (bf16[2048,128]{0,1:T(8,128)(2,1)S(1)}, bf16[2048,128]{0,1:T(8,128)(2,1)}, u32[]{:S(2)}, u32[]{:S(2)}) collective-permute-start(bf16[2048,128]{0,1:T(8,128)(2,1)S(1)} %get-tuple-element.11), channel_id=1, source_target_pairs={{0,4},{1,5},{2,6},{3,7},{4,0},{5,1},{6,2},{7,3},{8,12},{9,13},{10,... | collective-permute-start | bytes 1572872 | tf_op jit(solution)/shard_map/ppermute | solution.py:48
  194.7 51.9 %collective-permute-start.5 = (bf16[2048,128]{0,1:T(8,128)(2,1)S(1)}, bf16[2048,128]{0,1:T(8,128)(2,1)}, u32[]{:S(2)}, u32[]{:S(2)}) collective-permute-start(bf16[2048,128]{0,1:T(8,128)(2,1)S(1)} %get-tuple-element.10), channel_id=1, source_target_pairs={{0,5},{1,6},{2,7},{3,0},{4,1},{5,2},{6,3},{7,4},{8,13},{9,14},{10,... | collective-permute-start | bytes 1572872 | tf_op jit(solution)/shard_map/ppermute | solution.py:48
  205.5 41.2 %collective-permute-start.6 = (bf16[2048,128]{0,1:T(8,128)(2,1)S(1)}, bf16[2048,128]{0,1:T(8,128)(2,1)}, u32[]{:S(2)}, u32[]{:S(2)}) collective-permute-start(bf16[2048,128]{0,1:T(8,128)(2,1)S(1)} %get-tuple-element.9), channel_id=1, source_target_pairs={{0,6},{1,7},{2,0},{3,1},{4,2},{5,3},{6,4},{7,5},{8,14},{9,15},{10,... | collective-permute-start | bytes 1572872 | tf_op jit(solution)/shard_map/ppermute | solution.py:48
  212.4 41.1 %collective-permute-start.7 = (bf16[2048,128]{0,1:T(8,128)(2,1)S(1)}, bf16[2048,128]{0,1:T(8,128)(2,1)}, u32[]{:S(2)}, u32[]{:S(2)}) collective-permute-start(bf16[2048,128]{0,1:T(8,128)(2,1)S(1)} %get-tuple-element.8), channel_id=1, source_target_pairs={{0,7},{1,0},{2,1},{3,2},{4,3},{5,4},{6,5},{7,6},{8,15},{9,8},{10,9... | collective-permute-start | bytes 1572872 | tf_op jit(solution)/shard_map/ppermute | solution.py:48
Sparse Core Ops, SparseCore 0:
  10.3 60.8 all-gather.7
  72.9 37.2 all-gather.9
  112.4 80.9 all-gather.5

commit v7 on v4

--- a/solution.py
+++ b/solution.py
@@ -1,9 +1,11 @@
 import jax
 import jax.numpy as jnp
 from jax import lax
+from jax.sharding import Mesh
 from jax.sharding import PartitionSpec as P
 
 BLK = 128
+ROW = ("rx", "rz", "rc")
 
 
 def mask_blocks(data, mask):
@@ -26,8 +28,8 @@
         masked_c = mask_blocks(coeffs, coeff_mask)
         rows, width = masked_c.shape
         own_rows = lax.all_gather(masked_c, "col", axis=1, tiled=True)
-        moved = lax.ppermute(masked_c, ("row", "col"), perm)
-        gathered = lax.all_gather(moved, "row", axis=0, tiled=False)
+        moved = lax.ppermute(masked_c, ROW + ("col",), perm)
+        gathered = lax.all_gather(moved, ROW, axis=0, tiled=False)
         group_c = gathered.reshape(ratio, n_col, rows, width)
         masked_s = mask_blocks(intersection, intersection_mask).reshape(rows, ratio, rows)
         pieces = jnp.einsum(
@@ -47,18 +49,25 @@
             own_rows, both, (((0,), (0,)), ((), ())), preferred_element_type=jnp.float32
         )
         partial = partial[:, :width] + partial[:, width:]
-        spread = partial.reshape(n_row, -1, width)
-        spread = lax.all_to_all(spread, "row", 0, 0, tiled=True)
-        return jnp.sum(spread, axis=0)
+        core = lax.axis_index("rc")
+        spread = partial.reshape(n_row // 2, 2, -1, width)
+        keep = lax.dynamic_index_in_dim(spread, core, 1, keepdims=False)
+        give = lax.dynamic_index_in_dim(spread, 1 - core, 1, keepdims=False)
+        keep = keep + lax.ppermute(give, "rc", [(0, 1), (1, 0)])
+        keep = lax.all_to_all(keep, ("rx", "rz"), 0, 0, tiled=True)
+        return jnp.sum(keep, axis=0)
 
     return local
 
 
 def solution(mesh):
+    n_row, n_col = mesh.shape["row"], mesh.shape["col"]
+    fine = Mesh(mesh.devices.reshape(n_row // 4, 2, 2, n_col), ROW + ("col",))
+    spec = P(ROW, "col")
     return jax.shard_map(
-        make_local(mesh.shape["row"], mesh.shape["col"]),
-        mesh=mesh,
-        in_specs=(P("row", "col"), P("row", "col"), P("row", "col"), P("row", "col")),
-        out_specs=P("row", "col"),
+        make_local(n_row, n_col),
+        mesh=fine,
+        in_specs=(spec, spec, spec, spec),
+        out_specs=spec,
         check_vma=False,
     )

time: 233 us -> 231 us (level)
  blocking collectives: 16.6 us -> 12.9 us
    all_to_all x1, blocking collectives: 16.6 us -> 12.9 us  [local(): keep = lax.all_to_all(keep, ('rx', 'rz'), 0, 0, tiled=True)]
  transfers between devices with their start and end apart: 10 -> 11, of which waited for: 7 -> 8; matrix products, arithmetic and copies ran while one was open for 30% -> 30% of each run, Pallas kernels for 0% -> 0%
where the time goes in v7:
time: 231 us; the launch traced here: 229 us
  waiting for transfers between devices  80.1 us (35%)
  starting transfers between devices  41.6 us (18%)
  local copies, waits for them, and re-layouts  37.6 us (16%)
  matrix products  29.9 us (13%)
  between operations  13.5 us (6%)
  other arithmetic  13.1 us (6%)
  blocking collectives  12.9 us (6%)
    ppermute x7, starting transfers between devices, local(): got = lax.ppermute(out, 'col', [(c, (c + k) % n_col) for c in range(n_col)])  40.7 us
    all_gather x1, waiting for transfers between devices, local(): gathered = lax.all_gather(moved, ROW, axis=0, tiled=False)  33.9 us
    ppermute x7, waiting for transfers between devices, local(): got = lax.ppermute(out, 'col', [(c, (c + k) % n_col) for c in range(n_col)])  33.2 us
    mul x3, local copies, waits for them, and re-layouts, mask_blocks(): shaped * mask.astype(data.dtype)[:, None, :, None]  30.7 us
    dot_general x1, matrix products, local(): jnp.einsum('rhk,hokn->orn', masked_s, group_c, preferred_element_type=jnp...  26.4 us
    all_to_all x1, blocking collectives, local(): keep = lax.all_to_all(keep, ('rx', 'rz'), 0, 0, tiled=True)  12.9 us
    all_gather x1, waiting for transfers between devices, local(): own_rows = lax.all_gather(masked_c, 'col', axis=1, tiled=True)  10.8 us
    mul x3, other arithmetic, mask_blocks(): shaped * mask.astype(data.dtype)[:, None, :, None]  9.04 us
  transfers between devices with their start and end apart: 11, of which 8 were waited for; matrix products, arithmetic and copies ran while one was open for 30% of the time, Pallas kernels for 0%

profile of v7, /device:TPU:0, one launch (start us, length us, event | category | flops | bytes accessed | tf_op | source)
XLA Modules:
  0.0 228.7 jit_solution(7598955403014450598)
XLA Ops:
  6.5 0.0 all-gather.6.cloned.1.call-start
  6.5 0.7 convert_bitcast_fusion
  7.2 0.1 broadcast_bitcast_fusion
  7.3 1.4 broadcast_multiply_fusion
  8.7 0.0 copy-start.2
  8.7 0.7 collective-permute-start
  9.4 0.0 collective-permute-done
  9.4 0.0 copy-start.3
  9.4 0.8 copy-done.3
  10.2 0.0 all-gather.6.cloned.1.call-update
  10.2 0.0 all-gather.4.cloned.1.call-start
  10.3 0.0 copy-done.2
  10.3 0.7 all-gather.4.cloned.1.call-update
  11.0 0.7 convert_element_type.47
  11.7 0.0 copy-start
  11.7 2.8 %mul.36 = bf16[16,128,32,128]{3,2,1,0:T(8,128)(2,1)S(1)} broadcast(bf16[16,32]{1,0:T(8,128)(2,1)S(1)} %convert_element_type.47), dimensions={0,2} | broadcast | bytes 16778240 | tf_op jit(solution)/shard_map/mul | solution.py:14
  14.5 2.9 %copy-done = bf16[2048,4096]{1,0:T(8,128)(2,1)S(1)} copy-done((bf16[2048,4096]{1,0:T(8,128)(2,1)S(1)}, bf16[2048,4096]{1,0:T(8,128)(2,1)}, u32[]{:S(2)}) %copy-start) | copy-done | bytes 16777240
  17.4 7.0 %bitcast_multiply_fusion = bf16[2048,4096]{1,0:T(8,128)(2,1)} fusion(bf16[2048,4096]{1,0:T(8,128)(2,1)S(1)} %copy-done, bf16[256,8,32,128]{3,2,1,0:T(8,128)(2,1)S(1)} %bitcast.64), kind=kLoop, calls=%fused_computation | loop fusion | flops 8388608 | bytes 50331648 | tf_op jit(solution)/shard_map/mul | solution.py:14
  24.4 27.8 %mul.39 = bf16[2048,2,2048]{2,1,0:T(2,128)(2,1)} reshape(bf16[2048,4096]{1,0:T(8,128)(2,1)} %bitcast_multiply_fusion) | data formatting | bytes 33554432 | tf_op jit(solution)/shard_map/mul | solution.py:14
  52.2 33.9 %all-gather.6.cloned.1.call-done = bf16[32768,128]{1,0:T(8,128)(2,1)} async-done(((bf16[2048,128]{1,0:T(8,128)(2,1)}), bf16[32768,128]{1,0:T(8,128)(2,1)}) %all-gather.6.cloned.1.call-update) | async-done | bytes 8388624 | tf_op jit(solution)/shard_map/all_gather | solution.py:32
  86.1 26.4 %bitcast_convert_fusion = bf16[8,128,2048]{2,1,0:T(8,128)(2,1)S(1)} fusion(bf16[2,8,2048,128]{3,2,1,0:T(8,128)(2,1)} %bitcast.68, bf16[2048,2,2048,1]{2,1,0,3:T(2,128)(2,1)} %bitcast.65), kind=kOutput, calls=%fused_computation.3 | convolution fusion | flops 17181966336 | bytes 29360128 | tf_op jit(solution)/shard_map/rhk,hokn->orn/dot_general | solution.py:35
  112.5 0.0 copy-start.1
  112.5 1.9 copy-done.1
  114.5 1.2 dynamic-slice_bitcast_fusion.6
  115.7 3.0 %collective-permute-start.1 = (bf16[2048,128]{0,1:T(8,128)(2,1)S(1)}, bf16[2048,128]{0,1:T(8,128)(2,1)S(1)}, u32[]{:S(2)}, u32[]{:S(2)}) collective-permute-start(bf16[2048,128]{0,1:T(8,128)(2,1)S(1)} %get-tuple-element.7), channel_id=1, source_target_pairs={{0,1},{1,2},{2,3},{3,4},{4,5},{5,6},{6,7},{7,0},{8,9},{9,10},{10,1... | collective-permute-start | bytes 1572872 | tf_op jit(solution)/shard_map/ppermute | solution.py:42
  118.7 1.5 collective-permute-start.2
  120.2 2.1 collective-permute-start.3
  122.3 2.0 collective-permute-start.4
  124.3 4.5 %collective-permute-start.5 = (bf16[2048,128]{0,1:T(8,128)(2,1)S(1)}, bf16[2048,128]{0,1:T(8,128)(2,1)}, u32[]{:S(2)}, u32[]{:S(2)}) collective-permute-start(bf16[2048,128]{0,1:T(8,128)(2,1)S(1)} %get-tuple-element.10), channel_id=1, source_target_pairs={{0,5},{1,6},{2,7},{3,0},{4,1},{5,2},{6,3},{7,4},{8,13},{9,14},{10,... | collective-permute-start | bytes 1572872 | tf_op jit(solution)/shard_map/ppermute | solution.py:42
  128.9 9.5 %collective-permute-done.1 = bf16[2048,128]{0,1:T(8,128)(2,1)S(1)} collective-permute-done((bf16[2048,128]{0,1:T(8,128)(2,1)S(1)}, bf16[2048,128]{0,1:T(8,128)(2,1)S(1)}, u32[]{:S(2)}, u32[]{:S(2)}) %collective-permute-start.1) | collective-permute-done | bytes 524320 | tf_op jit(solution)/shard_map/ppermute | solution.py:42
  138.3 7.4 %collective-permute-start.6 = (bf16[2048,128]{0,1:T(8,128)(2,1)S(1)}, bf16[2048,128]{0,1:T(8,128)(2,1)}, u32[]{:S(2)}, u32[]{:S(2)}) collective-permute-start(bf16[2048,128]{0,1:T(8,128)(2,1)S(1)} %get-tuple-element.9), channel_id=1, source_target_pairs={{0,6},{1,7},{2,0},{3,1},{4,2},{5,3},{6,4},{7,5},{8,14},{9,15},{10,... | collective-permute-start | bytes 1572872 | tf_op jit(solution)/shard_map/ppermute | solution.py:42
  145.7 0.0 collective-permute-done.2
  145.7 20.2 %collective-permute-start.7 = (bf16[2048,128]{0,1:T(8,128)(2,1)S(1)}, bf16[2048,128]{0,1:T(8,128)(2,1)}, u32[]{:S(2)}, u32[]{:S(2)}) collective-permute-start(bf16[2048,128]{0,1:T(8,128)(2,1)S(1)} %get-tuple-element.8), channel_id=1, source_target_pairs={{0,7},{1,0},{2,1},{3,2},{4,3},{5,4},{6,5},{7,6},{8,15},{9,8},{10,9... | collective-permute-start | bytes 1572872 | tf_op jit(solution)/shard_map/ppermute | solution.py:42
  165.9 6.4 %collective-permute-done.3 = bf16[2048,128]{0,1:T(8,128)(2,1)} collective-permute-done((bf16[2048,128]{0,1:T(8,128)(2,1)}, bf16[2048,128]{0,1:T(8,128)(2,1)}, u32[]{:S(2)}, u32[]{:S(2)}) %collective-permute-start.3) | collective-permute-done | bytes 524320 | tf_op jit(solution)/shard_map/ppermute | solution.py:42
  172.3 1.4 collective-permute-done.4
  173.7 13.1 %collective-permute-done.5 = bf16[2048,128]{0,1:T(8,128)(2,1)} collective-permute-done((bf16[2048,128]{0,1:T(8,128)(2,1)S(1)}, bf16[2048,128]{0,1:T(8,128)(2,1)}, u32[]{:S(2)}, u32[]{:S(2)}) %collective-permute-start.5) | collective-permute-done | bytes 524320 | tf_op jit(solution)/shard_map/ppermute | solution.py:42
  186.9 0.0 collective-permute-done.6
  186.9 2.8 %collective-permute-done.7 = bf16[2048,128]{0,1:T(8,128)(2,1)} collective-permute-done((bf16[2048,128]{0,1:T(8,128)(2,1)S(1)}, bf16[2048,128]{0,1:T(8,128)(2,1)}, u32[]{:S(2)}, u32[]{:S(2)}) %collective-permute-start.7) | collective-permute-done | bytes 524320 | tf_op jit(solution)/shard_map/ppermute | solution.py:42
  189.6 2.5 %reduce-precision_convert_fusion = (bf16[2048,128]{0,1:T(8,128)(2,1)S(1)}, f32[2048,128]{0,1:T(8,128)S(1)}) fusion(bf16[2048,128]{0,1:T(8,128)(2,1)} %collective-permute-done.7, bf16[2048,128]{0,1:T(8,128)(2,1)} %collective-permute-done.6, bf16[2048,128]{0,1:T(8,128)(2,1)} %collective-permute-done.5, bf16[2048,128]{0,1:T(8,128)(2,1)} %collective-permute-done.4, ...), kind=kLoop, calls=%fused_computation.5 | loop fusion | flops 4456448 | bytes 5767172 | tf_op jit(solution)/shard_map/convert_element_type | solution.py:45
  192.2 0.1 fusion.4
  192.3 10.8 %all-gather.4.cloned.1.call-done = bf16[2048,1024]{1,0:T(8,128)(2,1)} async-done(((bf16[2048,128]{1,0:T(8,128)(2,1)}), bf16[2048,1024]{1,0:T(8,128)(2,1)}) %all-gather.4.cloned.1.call-update) | async-done | bytes 4194320 | tf_op jit(solution)/shard_map/all_gather | solution.py:30
  203.1 3.5 %fusion.5 = f32[1024,256]{1,0:T(8,128)S(1)} fusion(bf16[2048,1024]{1,0:T(8,128)(2,1)} %all-gather.4.cloned.1.call-done, bf16[2048,128]{0,1:T(8,128)(2,1)S(1)} %fusion.4, bf16[2048,128]{0,1:T(8,128)(2,1)S(1)} %get-tuple-element.5), kind=kOutput, calls=%fused_computation.7 | convolution fusion | flops 1075838976 | bytes 6291456 | tf_op jit(solution)/shard_map/dot_general | solution.py:48
  206.6 0.1 slice_add_fusion
  206.7 0.1 collective-permute-start.8
  206.7 1.5 collective-permute-done.8
  208.3 12.9 %all_to_all.5 = f32[8,64,128]{2,1,0:T(8,128)S(1)} all-to-all(f32[8,64,128]{2,1,0:T(8,128)S(1)} %bitcast_add_fusion.1), channel_id=1, replica_groups=mesh['rx'=4,'rz'=2,'rc'=2,'col'=8] {'rx','rz'}, dimensions={0} | all-to-all | bytes 524288 | tf_op jit(solution)/shard_map/all_to_all | solution.py:57
  221.2 0.6 reduce_sum.9
  (2 shorter events, 0.1 us)
Async XLA Ops:
  6.5 79.6 %all-gather.6.cloned.1.call-start = ((), (), s32[]{:S(2)}) async-start(), calls=%async_computation.2 | async-start | bytes 8912896 | tf_op jit(solution)/shard_map/all_gather | solution.py:32
  8.7 1.6 copy-start.2
  8.7 0.7 collective-permute-start
  9.4 0.8 copy-start.3
  10.2 192.9 %all-gather.4.cloned.1.call-start = ((), (), s32[]{:S(2)}) async-start(), calls=%async_computation.1 | async-start | bytes 4718592 | tf_op jit(solution)/shard_map/all_gather | solution.py:30
  11.7 5.8 %copy-start = (bf16[2048,4096]{1,0:T(8,128)(2,1)S(1)}, bf16[2048,4096]{1,0:T(8,128)(2,1)}, u32[]{:S(2)}) copy-start(bf16[2048,4096]{1,0:T(8,128)(2,1)} %param.5) | copy-start | bytes 50331652
  112.5 2.0 copy-start.1
  115.7 22.6 %collective-permute-start.1 = (bf16[2048,128]{0,1:T(8,128)(2,1)S(1)}, bf16[2048,128]{0,1:T(8,128)(2,1)S(1)}, u32[]{:S(2)}, u32[]{:S(2)}) collective-permute-start(bf16[2048,128]{0,1:T(8,128)(2,1)S(1)} %get-tuple-element.7), channel_id=1, source_target_pairs={{0,1},{1,2},{2,3},{3,4},{4,5},{5,6},{6,7},{7,0},{8,9},{9,10},{10,1... | collective-permute-start | bytes 1572872 | tf_op jit(solution)/shard_map/ppermute | solution.py:42
  118.7 27.0 %collective-permute-start.2 = (bf16[2048,128]{0,1:T(8,128)(2,1)S(1)}, bf16[2048,128]{0,1:T(8,128)(2,1)S(1)}, u32[]{:S(2)}, u32[]{:S(2)}) collective-permute-start(bf16[2048,128]{0,1:T(8,128)(2,1)S(1)} %get-tuple-element.13), channel_id=1, source_target_pairs={{0,2},{1,3},{2,4},{3,5},{4,6},{5,7},{6,0},{7,1},{8,10},{9,11},{10,... | collective-permute-start | bytes 1572872 | tf_op jit(solution)/shard_map/ppermute | solution.py:42
  120.2 52.2 %collective-permute-start.3 = (bf16[2048,128]{0,1:T(8,128)(2,1)}, bf16[2048,128]{0,1:T(8,128)(2,1)}, u32[]{:S(2)}, u32[]{:S(2)}) collective-permute-start(bf16[2048,128]{0,1:T(8,128)(2,1)} %get-tuple-element.12), channel_id=1, source_target_pairs={{0,3},{1,4},{2,5},{3,6},{4,7},{5,0},{6,1},{7,2},{8,11},{9,12},{10,... | collective-permute-start | bytes 1572872 | tf_op jit(solution)/shard_map/ppermute | solution.py:42
  122.3 51.4 %collective-permute-start.4 = (bf16[2048,128]{0,1:T(8,128)(2,1)S(1)}, bf16[2048,128]{0,1:T(8,128)(2,1)}, u32[]{:S(2)}, u32[]{:S(2)}) collective-permute-start(bf16[2048,128]{0,1:T(8,128)(2,1)S(1)} %get-tuple-element.11), channel_id=1, source_target_pairs={{0,4},{1,5},{2,6},{3,7},{4,0},{5,1},{6,2},{7,3},{8,12},{9,13},{10,... | collective-permute-start | bytes 1572872 | tf_op jit(solution)/shard_map/ppermute | solution.py:42
  124.3 62.6 %collective-permute-start.5 = (bf16[2048,128]{0,1:T(8,128)(2,1)S(1)}, bf16[2048,128]{0,1:T(8,128)(2,1)}, u32[]{:S(2)}, u32[]{:S(2)}) collective-permute-start(bf16[2048,128]{0,1:T(8,128)(2,1)S(1)} %get-tuple-element.10), channel_id=1, source_target_pairs={{0,5},{1,6},{2,7},{3,0},{4,1},{5,2},{6,3},{7,4},{8,13},{9,14},{10,... | collective-permute-start | bytes 1572872 | tf_op jit(solution)/shard_map/ppermute | solution.py:42
  138.3 48.5 %collective-permute-start.6 = (bf16[2048,128]{0,1:T(8,128)(2,1)S(1)}, bf16[2048,128]{0,1:T(8,128)(2,1)}, u32[]{:S(2)}, u32[]{:S(2)}) collective-permute-start(bf16[2048,128]{0,1:T(8,128)(2,1)S(1)} %get-tuple-element.9), channel_id=1, source_target_pairs={{0,6},{1,7},{2,0},{3,1},{4,2},{5,3},{6,4},{7,5},{8,14},{9,15},{10,... | collective-permute-start | bytes 1572872 | tf_op jit(solution)/shard_map/ppermute | solution.py:42
  145.7 43.9 %collective-permute-start.7 = (bf16[2048,128]{0,1:T(8,128)(2,1)S(1)}, bf16[2048,128]{0,1:T(8,128)(2,1)}, u32[]{:S(2)}, u32[]{:S(2)}) collective-permute-start(bf16[2048,128]{0,1:T(8,128)(2,1)S(1)} %get-tuple-element.8), channel_id=1, source_target_pairs={{0,7},{1,0},{2,1},{3,2},{4,3},{5,4},{6,5},{7,6},{8,15},{9,8},{10,9... | collective-permute-start | bytes 1572872 | tf_op jit(solution)/shard_map/ppermute | solution.py:42
  206.7 1.6 collective-permute-start.8
Sparse Core Ops, SparseCore 0:
  10.3 75.7 all-gather.5
  88.3 114.7 all-gather.3

commit v8 on v7

--- a/solution.py
+++ b/solution.py
@@ -21,7 +21,7 @@
     for src_r in range(n_row):
         for o in range(n_col):
             g, h = divmod(src_r, ratio)
-            dst_r = h * n_col + o
+            dst_r = o * ratio + h
             perm.append((src_r * n_col + o, dst_r * n_col + g))
 
     def local(coeffs, intersection, coeff_mask, intersection_mask):
@@ -30,10 +30,11 @@
         own_rows = lax.all_gather(masked_c, "col", axis=1, tiled=True)
         moved = lax.ppermute(masked_c, ROW + ("col",), perm)
         gathered = lax.all_gather(moved, ROW, axis=0, tiled=False)
-        group_c = gathered.reshape(ratio, n_col, rows, width)
-        masked_s = mask_blocks(intersection, intersection_mask).reshape(rows, ratio, rows)
+        group_c = gathered.reshape(n_col, ratio * rows, width)
+        masked_s, _ = lax.optimization_barrier(
+            (mask_blocks(intersection, intersection_mask), moved))
         pieces = jnp.einsum(
-            "rhk,hokn->orn", masked_s, group_c, preferred_element_type=jnp.float32
+            "rk,okn->orn", masked_s, group_c, preferred_element_type=jnp.float32
         ).astype(jnp.bfloat16)
         me = lax.axis_index("col")
         summed = lax.dynamic_index_in_dim(pieces, me, 0, keepdims=False).astype(jnp.float32)

time: 231 us -> 233 us (level)
  waiting for transfers between devices: 80.1 us -> 120 us
  local copies, waits for them, and re-layouts: 37.6 us -> 9.81 us
  starting transfers between devices: 41.6 us -> 36.3 us
  matrix products: 29.9 us -> 26.4 us
    all_gather x1, waiting for transfers between devices: 33.9 us -> 68.1 us  [local(): gathered = lax.all_gather(moved, ROW, axis=0, tiled=False)]
    mul x3 -> x2, local copies, waits for them, and re-layouts: 30.7 us -> 2.89 us  [mask_blocks(): shaped * mask.astype(data.dtype)[:, None, :, None]]
    ppermute x7, waiting for transfers between devices: 33.2 us -> 38.5 us  [local(): got = lax.ppermute(out, 'col', [(c, (c + k) % n_col) for c in range(n_col)])]
    ppermute x7, starting transfers between devices: 40.7 us -> 35.5 us  [local(): got = lax.ppermute(out, 'col', [(c, (c + k) % n_col) for c in range(n_col)])]
    dot_general x1, matrix products: 26.4 us -> 22.9 us  [local(): jnp.einsum('rk,okn->orn', masked_s, group_c, preferred_element_type=jnp.f...]
  transfers between devices with their start and end apart: 11 -> 11, of which waited for: 8 -> 7; matrix products, arithmetic and copies ran while one was open for 30% -> 16% of each run, Pallas kernels for 0% -> 0%
where the time goes in v8:
time: 233 us; the launch traced here: 231 us
  waiting for transfers between devices  120 us (52%)
  starting transfers between devices  36.3 us (16%)
  matrix products  26.4 us (11%)
  between operations  13.5 us (6%)
  other arithmetic  13.1 us (6%)
  blocking collectives  11.9 us (5%)
  local copies, waits for them, and re-layouts  9.81 us (4%)
    all_gather x1, waiting for transfers between devices, local(): gathered = lax.all_gather(moved, ROW, axis=0, tiled=False)  68.1 us
    ppermute x7, waiting for transfers between devices, local(): got = lax.ppermute(out, 'col', [(c, (c + k) % n_col) for c in range(n_col)])  38.5 us
    ppermute x7, starting transfers between devices, local(): got = lax.ppermute(out, 'col', [(c, (c + k) % n_col) for c in range(n_col)])  35.5 us
    dot_general x1, matrix products, local(): jnp.einsum('rk,okn->orn', masked_s, group_c, preferred_element_type=jnp.f...  22.9 us
    all_to_all x1, blocking collectives, local(): keep = lax.all_to_all(keep, ('rx', 'rz'), 0, 0, tiled=True)  11.9 us
    all_gather x1, waiting for transfers between devices, local(): own_rows = lax.all_gather(masked_c, 'col', axis=1, tiled=True)  11.7 us
    mul x3, other arithmetic, mask_blocks(): shaped * mask.astype(data.dtype)[:, None, :, None]  9.02 us
    unnamed x8, local copies, waits for them, and re-layouts  5.7 us
  transfers between devices with their start and end apart: 11, of which 7 were waited for; matrix products, arithmetic and copies ran while one was open for 16% of the time, Pallas kernels for 0%

profile of v8, /device:TPU:0, one launch (start us, length us, event | category | flops | bytes accessed | tf_op | source)
XLA Modules:
  0.0 231.5 jit_solution(5408000455179836508)
XLA Ops:
  6.5 0.0 all-gather.6.cloned.1.call-start
  6.5 0.7 convert_bitcast_fusion
  7.2 0.1 broadcast_bitcast_fusion
  7.3 1.4 broadcast_multiply_fusion
  8.7 0.0 copy-start.2
  8.7 0.7 collective-permute-start
  9.4 0.0 collective-permute-done
  9.4 0.0 copy-start.3
  9.4 0.8 copy-done.3
  10.2 0.0 all-gather.6.cloned.1.call-update
  10.2 0.0 all-gather.4.cloned.1.call-start
  10.3 0.0 copy-done.2
  10.3 0.7 all-gather.4.cloned.1.call-update
  11.0 0.7 convert_element_type.47
  11.7 0.0 copy-start
  11.7 2.8 %mul.33 = bf16[16,128,32,128]{3,2,1,0:T(8,128)(2,1)S(1)} broadcast(bf16[16,32]{1,0:T(8,128)(2,1)S(1)} %convert_element_type.47), dimensions={0,2} | broadcast | bytes 16778240 | tf_op jit(solution)/shard_map/mul | solution.py:14
  14.5 2.9 %copy-done = bf16[2048,4096]{1,0:T(8,128)(2,1)S(1)} copy-done((bf16[2048,4096]{1,0:T(8,128)(2,1)S(1)}, bf16[2048,4096]{1,0:T(8,128)(2,1)}, u32[]{:S(2)}) %copy-start) | copy-done | bytes 16777240
  17.4 7.0 %bitcast_multiply_fusion = bf16[2048,4096]{1,0:T(8,128)(2,1)} fusion(bf16[2048,4096]{1,0:T(8,128)(2,1)S(1)} %copy-done, bf16[256,8,32,128]{3,2,1,0:T(8,128)(2,1)S(1)} %bitcast.66), kind=kLoop, calls=%fused_computation | loop fusion | flops 8388608 | bytes 50331648 | tf_op jit(solution)/shard_map/mul | solution.py:14
  24.4 68.1 %all-gather.6.cloned.1.call-done = bf16[32768,128]{1,0:T(8,128)(2,1)} async-done(((bf16[2048,128]{1,0:T(8,128)(2,1)}), bf16[32768,128]{1,0:T(8,128)(2,1)}) %all-gather.6.cloned.1.call-update) | async-done | bytes 8388624 | tf_op jit(solution)/shard_map/all_gather | solution.py:32
  92.5 22.9 %fusion.2 = bf16[8,128,2048]{2,1,0:T(8,128)(2,1)S(1)} fusion(bf16[8,4096,128]{2,1,0:T(8,128)(2,1)} %bitcast.69, bf16[2048,4096]{1,0:T(8,128)(2,1)} %bitcast_multiply_fusion), kind=kOutput, calls=%fused_computation.3 | convolution fusion | flops 17181966336 | bytes 29360128 | tf_op jit(solution)/shard_map/rk,okn->orn/dot_general | solution.py:36
  115.4 0.0 copy-start.1
  115.4 1.9 copy-done.1
  117.3 1.2 dynamic-slice_bitcast_fusion.6
  118.5 3.0 %collective-permute-start.1 = (bf16[2048,128]{0,1:T(8,128)(2,1)S(1)}, bf16[2048,128]{0,1:T(8,128)(2,1)S(1)}, u32[]{:S(2)}, u32[]{:S(2)}) collective-permute-start(bf16[2048,128]{0,1:T(8,128)(2,1)S(1)} %get-tuple-element.9), channel_id=1, source_target_pairs={{0,1},{1,2},{2,3},{3,4},{4,5},{5,6},{6,7},{7,0},{8,9},{9,10},{10,1... | collective-permute-start | bytes 1572872 | tf_op jit(solution)/shard_map/ppermute | solution.py:43
  121.5 1.5 collective-permute-start.2
  123.0 2.1 collective-permute-start.3
  125.1 2.0 collective-permute-start.4
  127.1 4.5 %collective-permute-start.5 = (bf16[2048,128]{0,1:T(8,128)(2,1)S(1)}, bf16[2048,128]{0,1:T(8,128)(2,1)}, u32[]{:S(2)}, u32[]{:S(2)}) collective-permute-start(bf16[2048,128]{0,1:T(8,128)(2,1)S(1)} %get-tuple-element.12), channel_id=1, source_target_pairs={{0,5},{1,6},{2,7},{3,0},{4,1},{5,2},{6,3},{7,4},{8,13},{9,14},{10,... | collective-permute-start | bytes 1572872 | tf_op jit(solution)/shard_map/ppermute | solution.py:43
  131.7 6.0 %collective-permute-done.1 = bf16[2048,128]{0,1:T(8,128)(2,1)S(1)} collective-permute-done((bf16[2048,128]{0,1:T(8,128)(2,1)S(1)}, bf16[2048,128]{0,1:T(8,128)(2,1)S(1)}, u32[]{:S(2)}, u32[]{:S(2)}) %collective-permute-start.1) | collective-permute-done | bytes 524320 | tf_op jit(solution)/shard_map/ppermute | solution.py:43
  137.7 10.8 %collective-permute-start.6 = (bf16[2048,128]{0,1:T(8,128)(2,1)S(1)}, bf16[2048,128]{0,1:T(8,128)(2,1)}, u32[]{:S(2)}, u32[]{:S(2)}) collective-permute-start(bf16[2048,128]{0,1:T(8,128)(2,1)S(1)} %get-tuple-element.11), channel_id=1, source_target_pairs={{0,6},{1,7},{2,0},{3,1},{4,2},{5,3},{6,4},{7,5},{8,14},{9,15},{10,... | collective-permute-start | bytes 1572872 | tf_op jit(solution)/shard_map/ppermute | solution.py:43
  148.5 0.0 collective-permute-done.2
  148.5 11.6 %collective-permute-start.7 = (bf16[2048,128]{0,1:T(8,128)(2,1)S(1)}, bf16[2048,128]{0,1:T(8,128)(2,1)}, u32[]{:S(2)}, u32[]{:S(2)}) collective-permute-start(bf16[2048,128]{0,1:T(8,128)(2,1)S(1)} %get-tuple-element.10), channel_id=1, source_target_pairs={{0,7},{1,0},{2,1},{3,2},{4,3},{5,4},{6,5},{7,6},{8,15},{9,8},{10,9... | collective-permute-start | bytes 1572872 | tf_op jit(solution)/shard_map/ppermute | solution.py:43
  160.0 17.1 %collective-permute-done.3 = bf16[2048,128]{0,1:T(8,128)(2,1)} collective-permute-done((bf16[2048,128]{0,1:T(8,128)(2,1)}, bf16[2048,128]{0,1:T(8,128)(2,1)}, u32[]{:S(2)}, u32[]{:S(2)}) %collective-permute-start.3) | collective-permute-done | bytes 524320 | tf_op jit(solution)/shard_map/ppermute | solution.py:43
  177.2 0.0 collective-permute-done.4
  177.2 11.6 %collective-permute-done.5 = bf16[2048,128]{0,1:T(8,128)(2,1)} collective-permute-done((bf16[2048,128]{0,1:T(8,128)(2,1)S(1)}, bf16[2048,128]{0,1:T(8,128)(2,1)}, u32[]{:S(2)}, u32[]{:S(2)}) %collective-permute-start.5) | collective-permute-done | bytes 524320 | tf_op jit(solution)/shard_map/ppermute | solution.py:43
  188.8 0.0 collective-permute-done.6
  188.8 3.7 %collective-permute-done.7 = bf16[2048,128]{0,1:T(8,128)(2,1)} collective-permute-done((bf16[2048,128]{0,1:T(8,128)(2,1)S(1)}, bf16[2048,128]{0,1:T(8,128)(2,1)}, u32[]{:S(2)}, u32[]{:S(2)}) %collective-permute-start.7) | collective-permute-done | bytes 524320 | tf_op jit(solution)/shard_map/ppermute | solution.py:43
  192.5 2.5 %reduce-precision_convert_fusion = (bf16[2048,128]{0,1:T(8,128)(2,1)S(1)}, f32[2048,128]{0,1:T(8,128)S(1)}) fusion(bf16[2048,128]{0,1:T(8,128)(2,1)} %collective-permute-done.7, bf16[2048,128]{0,1:T(8,128)(2,1)} %collective-permute-done.6, bf16[2048,128]{0,1:T(8,128)(2,1)} %collective-permute-done.5, bf16[2048,128]{0,1:T(8,128)(2,1)} %collective-permute-done.4, ...), kind=kLoop, calls=%fused_computation.5 | loop fusion | flops 4456448 | bytes 5767172 | tf_op jit(solution)/shard_map/convert_element_type | solution.py:46
  195.0 0.1 fusion.5
  195.1 11.7 %all-gather.4.cloned.1.call-done = bf16[2048,1024]{1,0:T(8,128)(2,1)} async-done(((bf16[2048,128]{1,0:T(8,128)(2,1)}), bf16[2048,1024]{1,0:T(8,128)(2,1)}) %all-gather.4.cloned.1.call-update) | async-done | bytes 4194320 | tf_op jit(solution)/shard_map/all_gather | solution.py:30
  206.8 3.5 %fusion.6 = f32[1024,256]{1,0:T(8,128)S(1)} fusion(bf16[2048,1024]{1,0:T(8,128)(2,1)} %all-gather.4.cloned.1.call-done, bf16[2048,128]{0,1:T(8,128)(2,1)S(1)} %fusion.5, bf16[2048,128]{0,1:T(8,128)(2,1)S(1)} %get-tuple-element.7), kind=kOutput, calls=%fused_computation.7 | convolution fusion | flops 1075838976 | bytes 6291456 | tf_op jit(solution)/shard_map/dot_general | solution.py:49
  210.3 0.1 slice_add_fusion
  210.4 0.1 collective-permute-start.8
  210.5 1.5 collective-permute-done.8
  212.1 11.9 %all_to_all.5 = f32[8,64,128]{2,1,0:T(8,128)S(1)} all-to-all(f32[8,64,128]{2,1,0:T(8,128)S(1)} %bitcast_add_fusion.1), channel_id=1, replica_groups=mesh['rx'=4,'rz'=2,'rc'=2,'col'=8] {'rx','rz'}, dimensions={0} | all-to-all | bytes 524288 | tf_op jit(solution)/shard_map/all_to_all | solution.py:58
  224.0 0.6 reduce_sum.9
  (2 shorter events, 0.1 us)
Async XLA Ops:
  6.5 85.9 %all-gather.6.cloned.1.call-start = ((), (), s32[]{:S(2)}) async-start(), calls=%async_computation.2 | async-start | bytes 8912896 | tf_op jit(solution)/shard_map/all_gather | solution.py:32
  8.7 1.6 copy-start.2
  8.7 0.7 collective-permute-start
  9.4 0.8 copy-start.3
  10.2 196.6 %all-gather.4.cloned.1.call-start = ((), (), s32[]{:S(2)}) async-start(), calls=%async_computation.1 | async-start | bytes 4718592 | tf_op jit(solution)/shard_map/all_gather | solution.py:30
  11.7 5.8 %copy-start = (bf16[2048,4096]{1,0:T(8,128)(2,1)S(1)}, bf16[2048,4096]{1,0:T(8,128)(2,1)}, u32[]{:S(2)}) copy-start(bf16[2048,4096]{1,0:T(8,128)(2,1)} %param.5) | copy-start | bytes 50331652
  115.4 2.0 copy-start.1
  118.5 19.1 %collective-permute-start.1 = (bf16[2048,128]{0,1:T(8,128)(2,1)S(1)}, bf16[2048,128]{0,1:T(8,128)(2,1)S(1)}, u32[]{:S(2)}, u32[]{:S(2)}) collective-permute-start(bf16[2048,128]{0,1:T(8,128)(2,1)S(1)} %get-tuple-element.9), channel_id=1, source_target_pairs={{0,1},{1,2},{2,3},{3,4},{4,5},{5,6},{6,7},{7,0},{8,9},{9,10},{10,1... | collective-permute-start | bytes 1572872 | tf_op jit(solution)/shard_map/ppermute | solution.py:43
  121.5 26.9 %collective-permute-start.2 = (bf16[2048,128]{0,1:T(8,128)(2,1)S(1)}, bf16[2048,128]{0,1:T(8,128)(2,1)S(1)}, u32[]{:S(2)}, u32[]{:S(2)}) collective-permute-start(bf16[2048,128]{0,1:T(8,128)(2,1)S(1)} %get-tuple-element.15), channel_id=1, source_target_pairs={{0,2},{1,3},{2,4},{3,5},{4,6},{5,7},{6,0},{7,1},{8,10},{9,11},{10,... | collective-permute-start | bytes 1572872 | tf_op jit(solution)/shard_map/ppermute | solution.py:43
  123.0 54.2 %collective-permute-start.3 = (bf16[2048,128]{0,1:T(8,128)(2,1)}, bf16[2048,128]{0,1:T(8,128)(2,1)}, u32[]{:S(2)}, u32[]{:S(2)}) collective-permute-start(bf16[2048,128]{0,1:T(8,128)(2,1)} %get-tuple-element.14), channel_id=1, source_target_pairs={{0,3},{1,4},{2,5},{3,6},{4,7},{5,0},{6,1},{7,2},{8,11},{9,12},{10,... | collective-permute-start | bytes 1572872 | tf_op jit(solution)/shard_map/ppermute | solution.py:43
  125.1 52.1 %collective-permute-start.4 = (bf16[2048,128]{0,1:T(8,128)(2,1)S(1)}, bf16[2048,128]{0,1:T(8,128)(2,1)}, u32[]{:S(2)}, u32[]{:S(2)}) collective-permute-start(bf16[2048,128]{0,1:T(8,128)(2,1)S(1)} %get-tuple-element.13), channel_id=1, source_target_pairs={{0,4},{1,5},{2,6},{3,7},{4,0},{5,1},{6,2},{7,3},{8,12},{9,13},{10,... | collective-permute-start | bytes 1572872 | tf_op jit(solution)/shard_map/ppermute | solution.py:43
  127.1 61.7 %collective-permute-start.5 = (bf16[2048,128]{0,1:T(8,128)(2,1)S(1)}, bf16[2048,128]{0,1:T(8,128)(2,1)}, u32[]{:S(2)}, u32[]{:S(2)}) collective-permute-start(bf16[2048,128]{0,1:T(8,128)(2,1)S(1)} %get-tuple-element.12), channel_id=1, source_target_pairs={{0,5},{1,6},{2,7},{3,0},{4,1},{5,2},{6,3},{7,4},{8,13},{9,14},{10,... | collective-permute-start | bytes 1572872 | tf_op jit(solution)/shard_map/ppermute | solution.py:43
  137.7 51.1 %collective-permute-start.6 = (bf16[2048,128]{0,1:T(8,128)(2,1)S(1)}, bf16[2048,128]{0,1:T(8,128)(2,1)}, u32[]{:S(2)}, u32[]{:S(2)}) collective-permute-start(bf16[2048,128]{0,1:T(8,128)(2,1)S(1)} %get-tuple-element.11), channel_id=1, source_target_pairs={{0,6},{1,7},{2,0},{3,1},{4,2},{5,3},{6,4},{7,5},{8,14},{9,15},{10,... | collective-permute-start | bytes 1572872 | tf_op jit(solution)/shard_map/ppermute | solution.py:43
  148.5 44.0 %collective-permute-start.7 = (bf16[2048,128]{0,1:T(8,128)(2,1)S(1)}, bf16[2048,128]{0,1:T(8,128)(2,1)}, u32[]{:S(2)}, u32[]{:S(2)}) collective-permute-start(bf16[2048,128]{0,1:T(8,128)(2,1)S(1)} %get-tuple-element.10), channel_id=1, source_target_pairs={{0,7},{1,0},{2,1},{3,2},{4,3},{5,4},{6,5},{7,6},{8,15},{9,8},{10,9... | collective-permute-start | bytes 1572872 | tf_op jit(solution)/shard_map/ppermute | solution.py:43
  210.4 1.6 collective-permute-start.8
Sparse Core Ops, SparseCore 0:
  10.3 82.1 all-gather.5
  94.7 112.1 all-gather.3
